TPU v7x, 256 devices: a whole 4x4x8 slice. The times are simulated.
256 devices in a mesh: chan: 64 (over z, x, y_lo), tm: 4 (over y_hi, core).
Axes of the slice: x: 4, y: 4 (y_hi: 2, y_lo: 2; y = y_hi * 2 + y_lo), z: 8, core: 2. Of those that a mesh axis runs over, the one named last changes fastest.
Arguments:
- raw_windows: bfloat16 [64, 4096, 2048], P('tm', 'chan'), may hold values from -480 to 480
- pairings: int32 [2, 64], replicated, may hold values from 0 to 63, as said below
Outputs:
- stacked_spectra: bfloat16 [2, 2, 4096, 64, 512], P(None, None, 'chan', None, 'tm')
Inputs may be any that keep to these rules, and one draw needn't show every extreme that they name: Each row pairs the 64 blocks: pairings[r, pairings[r, b]] = b and no block is its own partner.
All inputs are finite; a program needn't handle non-finite values.
Results may differ from a plain program's by a relative error of at most 0.0075.
Values may be sent and summed in bfloat16 or wider, within the bound.
No kernel may reach another device: no remote copies, remote signals or barrier semaphores. Data moves between devices by JAX's collectives and lax.ppermute only.
A program may use at most 192 MiB of HBM per device.

v0:
```python
import functools
import math

import jax
import jax.numpy as jnp
from jax import lax
from jax.experimental import pallas as pl
from jax.experimental.pallas import tpu as pltpu
from jax.sharding import PartitionSpec as P

F = 512
L = 2048
ROUNDS = 2


def band_table(chan_count, day_count):
    per_piece = F // (chan_count * day_count)
    row_ids = jnp.arange(2 * F, dtype=jnp.int32)
    piece_idx = row_ids // (day_count * 2 * per_piece)
    remainder = row_ids % (day_count * 2 * per_piece)
    group_idx = remainder // (2 * per_piece)
    within = remainder % (2 * per_piece)
    imag_flag = within // per_piece
    offset_idx = within % per_piece
    freq_ids = group_idx * (chan_count * per_piece) + offset_idx * chan_count + piece_idx
    lanes = 128
    hi_ids = jnp.arange(L // lanes, dtype=jnp.int32)
    lo_ids = jnp.arange(lanes, dtype=jnp.int32)
    two_pi = 2.0 * math.pi / L
    hi_angle = ((freq_ids[:, None] + 1) * (hi_ids[None, :] * lanes) % L).astype(jnp.float32) * two_pi
    lo_angle = ((freq_ids[:, None] + 1) * lo_ids[None, :] % L).astype(jnp.float32) * two_pi
    hi_cos, hi_sin = jnp.cos(hi_angle), jnp.sin(hi_angle)
    lo_cos, lo_sin = jnp.cos(lo_angle), jnp.sin(lo_angle)
    is_real = (imag_flag == 0)[:, None]
    first = jnp.where(is_real, hi_cos, -hi_sin)
    second = jnp.where(is_real, -hi_sin, -hi_cos)
    samples = jnp.arange(L, dtype=jnp.int32).reshape(L // lanes, lanes)
    taper_vals = 0.5 - 0.5 * jnp.cos((samples.astype(jnp.float32) + 0.5) * (2.0 * math.pi / L))
    values = (
        first[:, :, None] * lo_cos[:, None, :] + second[:, :, None] * lo_sin[:, None, :]
    ) * taper_vals[None]
    values = values.reshape(2 * F, L)
    return values.astype(jnp.bfloat16)


def pair_kernel(pair_ref, x_ref, o_ref, *, group, day_count, half, width, scale_value):
    step = pl.program_id(0)
    round_idx = pl.program_id(1)
    lane = lax.broadcasted_iota(jnp.int32, (width, 2 * width), 1)
    low_lanes = lane < width

    def body(k, carry):
        block = step * group + k
        partner = pair_ref[round_idx, block]
        acc_re = jnp.zeros((width, 2 * width), jnp.float32)
        acc_im = jnp.zeros((width, 2 * width), jnp.float32)
        for day in range(day_count):
            own = x_ref[block, day]
            other = x_ref[partner, day]
            rotated = jnp.concatenate([-other[half:], other[:half]], axis=0)
            both = jnp.concatenate([other, rotated], axis=1)
            prods = [
                lax.dot_general(
                    own[:, off * width:(off + 1) * width], both,
                    (((0,), (0,)), ((), ())), preferred_element_type=jnp.float32,
                )
                for off in range(2)
            ]
            re = jnp.where(low_lanes, prods[0][:, :2 * width], prods[1][:, :2 * width])
            im = jnp.where(low_lanes, prods[0][:, 2 * width:], prods[1][:, 2 * width:])
            acc_re += (re * scale_value).astype(jnp.bfloat16).astype(jnp.float32)
            acc_im += (im * scale_value).astype(jnp.bfloat16).astype(jnp.float32)
        o_ref[k, 0, 0] = acc_re.astype(jnp.bfloat16)
        o_ref[k, 0, 1] = acc_im.astype(jnp.bfloat16)
        return carry

    lax.fori_loop(0, group, body, 0)


def pair_stage(pairings, spectra, scale_value):
    block_count, day_count, rows, lanes = spectra.shape
    width = lanes // 2
    group = 8
    kernel = functools.partial(
        pair_kernel, group=group, day_count=day_count, half=rows // 2, width=width,
        scale_value=scale_value,
    )
    return pl.pallas_call(
        kernel,
        grid_spec=pltpu.PrefetchScalarGridSpec(
            num_scalar_prefetch=1,
            grid=(block_count // group, ROUNDS),
            in_specs=[pl.BlockSpec(spectra.shape, lambda i, r, pr: (0, 0, 0, 0))],
            out_specs=pl.BlockSpec(
                (group, 1, 2, width, lanes), lambda i, r, pr: (i, r, 0, 0, 0)
            ),
        ),
        out_shape=jax.ShapeDtypeStruct((block_count, ROUNDS, 2, width, lanes), jnp.bfloat16),
    )(pairings, spectra)


def on_device(raw_windows, pairings):
    win_count, block_width, length = raw_windows.shape
    chan_count = lax.axis_size("chan")
    day_count = lax.axis_size("tm")
    per_piece = F // (chan_count * day_count)
    dft_table = band_table(chan_count, day_count)
    flat_raw = raw_windows.reshape(win_count * block_width, length)
    spectra = lax.dot_general(
        dft_table, flat_raw, (((1,), (1,)), ((), ())), preferred_element_type=jnp.float32
    )
    power_sum = jnp.sum(spectra * spectra, axis=0) / F
    whitened = (spectra * lax.rsqrt(power_sum + 1e-06)[None, :]).astype(jnp.bfloat16)
    layered = whitened.reshape(1, chan_count, day_count, 2 * per_piece, win_count * block_width)
    banded = lax.all_to_all(layered, "chan", split_axis=1, concat_axis=0, tiled=True)
    scale_value = 1.0 / math.sqrt(win_count * day_count)
    pooled = lax.all_to_all(banded, "tm", split_axis=2, concat_axis=1, tiled=True)
    by_block = pooled.reshape(chan_count, day_count, 2, per_piece, win_count, block_width)
    by_block = jnp.transpose(by_block, (0, 1, 2, 4, 3, 5)).reshape(
        chan_count, day_count, 2 * win_count, per_piece * block_width
    )
    tiles = pair_stage(pairings, by_block, scale_value)
    received = lax.all_to_all(tiles, "chan", split_axis=0, concat_axis=0, tiled=True)
    received = received.reshape(chan_count, ROUNDS, 2, block_width, per_piece, block_width)
    stacked = jnp.transpose(received, (1, 2, 3, 5, 4, 0))
    return stacked.reshape(ROUNDS, 2, block_width, block_width, per_piece * chan_count)


def solution(mesh):
    return jax.shard_map(
        on_device,
        mesh=mesh,
        in_specs=(P("tm", "chan", None), P()),
        out_specs=P(None, None, "chan", None, "tm"),
        check_vma=False,
    )
```

profile of v0, /device:TPU:2, one launch (start us, length us, event | category | flops | bytes accessed | tf_op | source)
XLA Modules:
  0.0 346.2 jit_solution(2842457528540658220)
XLA Ops:
  0.0 0.1 multiply_subtract_fusion
  0.1 0.0 copy-start
  0.1 2.1 fusion.14
  2.2 2.2 fusion.12
  4.4 8.7 %multiply_convert_fusion = bf16[1024,16,128]{2,1,0:T(8,128)(2,1)S(1)} fusion(f32[16,128]{1,0:T(8,128)S(1)} %multiply_subtract_fusion, f32[1024,128]{1,0:T(8,128)S(1)} %get-tuple-element.8, f32[1024,16]{1,0:T(8,128)S(1)} %get-tuple-element.6, f32[1024,128]{1,0:T(8,128)S(1)} %get-tuple-element.7, f32[1024,16]{1,0:T(8,128)S(1)} %get-tuple-element.5), kind=kLoop, calls=%fused_computation | loop fusion | flops 10485760 | bytes 5382144 | tf_op jit(solution)/shard_map/convert_element_type | solution.py:43
  13.1 0.0 copy-done
  13.1 4.5 %multiply_reduce_fusion = (f32[1024]{0:T(1024)S(1)}, f32[1024,1024]{1,0:T(8,128)S(1)}) fusion(bf16[1024,2048]{1,0:T(8,128)(2,1)S(1)} %bitcast.23, bf16[128,8,16,128]{3,2,1,0:T(8,128)(2,1)S(1)} %bitcast.22), kind=kOutput, calls=%fused_computation.5 | convolution fusion | flops 4297063424 | bytes 12587008 | tf_op jit(solution)/shard_map/dot_general | solution.py:109
  17.7 1.9 multiply_convert_fusion.1
  19.6 2.7 reshape.335
  22.4 63.2 %all_to_all.26 = bf16[1,64,4,4,1024]{4,3,2,0,1:T(4,128)(2,1)S(1)} all-to-all(bf16[1,64,4,4,1024]{4,3,2,0,1:T(4,128)(2,1)S(1)} %bitcast.20), channel_id=1, replica_groups=mesh['chan'=64,'tm'=4] {'chan'}, dimensions={1} | all-to-all | bytes 4194304 | tf_op jit(solution)/shard_map/all_to_all | solution.py:115
  85.6 1.2 copy.8
  86.7 31.1 %all_to_all.27 = bf16[64,1,4,4,1024]{4,0,3,1,2:T(8,128)(2,1)S(1)} all-to-all(bf16[64,1,4,4,1024]{4,0,3,1,2:T(8,128)(2,1)S(1)} %copy.8), channel_id=1, replica_groups=mesh['chan'=64,'tm'=4] {'tm'}, dimensions={2} | all-to-all | bytes 4194304 | tf_op jit(solution)/shard_map/all_to_all | solution.py:117
  117.9 3.9 %reshape.336 = bf16[64,4,2,2,16,64]{5,4,0,3,2,1:T(8,128)(2,1)} reshape(bf16[64,1,4,4,1024]{4,0,3,1,2:T(8,128)(2,1)S(1)} %all_to_all.27) | data formatting | bytes 4194304 | tf_op jit(solution)/shard_map/reshape | solution.py:118
  121.8 10.6 %copy.9 = bf16[64,4,2,16,2,64]{5,4,3,2,1,0:T(2,128)(2,1)} copy(bf16[64,4,2,16,2,64]{5,3,0,4,2,1:T(8,128)(2,1)} %bitcast.19) | data formatting | bytes 4194304 | tf_op jit(solution)/shard_map/transpose | solution.py:119
  132.4 7.8 %reshape.337.x_ref = bf16[64,4,32,128]{3,2,1,0:T(8,128)(2,1)} reshape(bf16[64,4,2,16,2,64]{5,4,3,2,1,0:T(2,128)(2,1)} %copy.9) | data formatting | bytes 4194304 | tf_op jit(solution)/shard_map/reshape | solution.py:119
  140.2 46.1 %shard_map.28 = bf16[64,2,2,64,128]{4,3,2,1,0:T(8,128)(2,1)} custom-call(s32[2,64]{1,0:T(2,128)} %pair_ref.1, bf16[64,4,32,128]{3,2,1,0:T(8,128)(2,1)} %reshape.337.x_ref), custom_call_target="tpu_custom_call" | custom-call | tf_op jit(solution)/shard_map/pallas_call | solution.py:88
  186.3 101.9 %all_to_all.28 = bf16[64,2,2,64,128]{4,3,2,1,0:T(8,128)(2,1)} all-to-all(bf16[64,2,2,64,128]{4,3,2,1,0:T(8,128)(2,1)} %shard_map.28), channel_id=1, replica_groups=mesh['chan'=64,'tm'=4] {'chan'}, dimensions={0} | all-to-all | bytes 8388608 | tf_op jit(solution)/shard_map/all_to_all | solution.py:123
  288.2 14.7 %reshape.338 = bf16[64,2,2,64,2,64]{5,4,3,2,1,0:T(2,128)(2,1)} reshape(bf16[64,2,2,64,128]{4,3,2,1,0:T(8,128)(2,1)} %all_to_all.28) | data formatting | bytes 8388608 | tf_op jit(solution)/shard_map/reshape | solution.py:124
  302.9 29.1 %copy.10 = bf16[2,2,64,64,2,64]{5,4,3,2,1,0:T(2,128)(2,1)} copy(bf16[2,2,64,64,2,64]{3,4,2,1,0,5:T(2,128)(2,1)} %bitcast.18) | data formatting | bytes 8388608 | tf_op jit(solution)/shard_map/transpose | solution.py:125
  332.0 14.2 %reshape.339 = bf16[2,2,64,64,128]{4,3,2,1,0:T(8,128)(2,1)} reshape(bf16[2,2,64,64,2,64]{5,4,3,2,1,0:T(2,128)(2,1)} %copy.10) | data formatting | bytes 8388608 | tf_op jit(solution)/shard_map/reshape | solution.py:126
  (4 shorter events, 0.0 us)
Async XLA Ops:
  0.1 13.0 %copy-start = (bf16[16,64,2048]{2,1,0:T(8,128)(2,1)S(1)}, bf16[16,64,2048]{2,1,0:T(8,128)(2,1)}, u32[]{:S(2)}) copy-start(bf16[16,64,2048]{2,1,0:T(8,128)(2,1)} %param.2) | copy-start | bytes 12582916
where the time goes:
time: 348 us; the launch traced here: 346 us
  blocking collectives  196 us (56%)
  local copies, waits for them, and re-layouts  84.2 us (24%)
  Pallas kernels  46.1 us (13%)
  other arithmetic  15 us (4%)
  matrix products  4.54 us (1%)
    all_to_all x1, blocking collectives, on_device(): lax.all_to_all(tiles, 'chan', split_axis=0, concat_axis=0, tiled=True)  102 us
    all_to_all x1, blocking collectives, on_device(): lax.all_to_all(layered, 'chan', split_axis=1, concat_axis=0, tiled=True)  63.2 us
    pallas_call x1, Pallas kernels, pair_stage(): pl.pallas_call(kernel, grid_spec=pltpu.PrefetchScalarGridSpec(num_scalar_...  46.1 us
    all_to_all x1, blocking collectives, on_device(): lax.all_to_all(banded, 'tm', split_axis=2, concat_axis=1, tiled=True)  31.1 us
    transpose x1, local copies, waits for them, and re-layouts, on_device(): stacked = jnp.transpose(received, (1, 2, 3, 5, 4, 0))  29.1 us
    reshape x1, local copies, waits for them, and re-layouts, on_device(): received.reshape(chan_count, ROUNDS, 2, block_width, per_piece, block_width)  14.7 us
    reshape x1, local copies, waits for them, and re-layouts, on_device(): stacked.reshape(ROUNDS, 2, block_width, block_width, per_piece * chan_count)  14.2 us
    transpose x1, local copies, waits for them, and re-layouts, on_device(): jnp.transpose(by_block, (0, 1, 2, 4, 3, 5))  10.6 us

commit v1 on v0

--- a/solution.py
+++ b/solution.py
@@ -99,6 +99,25 @@
     )(pairings, spectra)
 
 
+def unshuffle_kernel(x_ref, o_ref, *, group, width):
+    for k in range(group):
+        flipped = x_ref[k].astype(jnp.float32).T
+        o_ref[k] = jnp.concatenate([flipped[:width], flipped[width:]], axis=1).astype(o_ref.dtype)
+
+
+def unshuffle_stage(received):
+    rows, sources, lanes = received.shape
+    group = 16
+    kernel = functools.partial(unshuffle_kernel, group=group, width=lanes // 2)
+    return pl.pallas_call(
+        kernel,
+        grid=(rows // group,),
+        in_specs=[pl.BlockSpec((group, sources, lanes), lambda i: (i, 0, 0))],
+        out_specs=pl.BlockSpec((group, lanes // 2, 2 * sources), lambda i: (i, 0, 0)),
+        out_shape=jax.ShapeDtypeStruct((rows, lanes // 2, 2 * sources), jnp.bfloat16),
+    )(received)
+
+
 def on_device(raw_windows, pairings):
     win_count, block_width, length = raw_windows.shape
     chan_count = lax.axis_size("chan")
@@ -120,11 +139,11 @@
         chan_count, day_count, 2 * win_count, per_piece * block_width
     )
     tiles = pair_stage(pairings, by_block, scale_value)
-    received = lax.all_to_all(tiles, "chan", split_axis=0, concat_axis=0, tiled=True)
-    received = received.reshape(chan_count, ROUNDS, 2, block_width, per_piece, block_width)
-    stacked = jnp.transpose(received, (1, 2, 3, 5, 4, 0))
+    rows = ROUNDS * 2 * block_width
+    tiles = tiles.reshape(chan_count, rows, 1, 2 * block_width)
+    received = lax.all_to_all(tiles, "chan", split_axis=0, concat_axis=2, tiled=True)
+    stacked = unshuffle_stage(received.reshape(rows, chan_count, 2 * block_width))
     return stacked.reshape(ROUNDS, 2, block_width, block_width, per_piece * chan_count)
-
 
 def solution(mesh):
     return jax.shard_map(

time: 348 us -> 306 us (0.88)
  local copies, waits for them, and re-layouts: 84.2 us -> 30.8 us
  Pallas kernels: 46.1 us -> 59.1 us
    transpose x1 -> x0, local copies, waits for them, and re-layouts: 29.1 us -> none  [on_device(): stacked = jnp.transpose(received, (1, 2, 3, 5, 4, 0))]
    reshape x2 -> x0, local copies, waits for them, and re-layouts: 28.9 us -> none  [the longest x1 14.7 us: on_device(): received.reshape(chan_count, ROUNDS, 2, block_width, per_piece, block_width)]
    pallas_call x0 -> x1, Pallas kernels: none -> 13 us  [unshuffle_stage(): pl.pallas_call(kernel, grid=(rows // group,), in_specs=[pl.BlockSpec((gro...]
    all_to_all x0 -> x1, local copies, waits for them, and re-layouts: none -> 4.63 us  [on_device(): lax.all_to_all(tiles, 'chan', split_axis=0, concat_axis=2, tiled=True)]
where the time goes in v1:
time: 306 us
  blocking collectives  196 us (64%)
  Pallas kernels  59.1 us (19%)
  local copies, waits for them, and re-layouts  30.8 us (10%)
  other arithmetic  15 us (5%)
  matrix products  4.54 us (1%)
    all_to_all x1, blocking collectives, on_device(): lax.all_to_all(tiles, 'chan', split_axis=0, concat_axis=2, tiled=True)  102 us
    all_to_all x1, blocking collectives, on_device(): lax.all_to_all(layered, 'chan', split_axis=1, concat_axis=0, tiled=True)  63.2 us
    pallas_call x1, Pallas kernels, pair_stage(): pl.pallas_call(kernel, grid_spec=pltpu.PrefetchScalarGridSpec(num_scalar_...  46.1 us
    all_to_all x1, blocking collectives, on_device(): lax.all_to_all(banded, 'tm', split_axis=2, concat_axis=1, tiled=True)  31.1 us
    pallas_call x1, Pallas kernels, unshuffle_stage(): pl.pallas_call(kernel, grid=(rows // group,), in_specs=[pl.BlockSpec((gro...  13 us
    transpose x1, local copies, waits for them, and re-layouts, on_device(): jnp.transpose(by_block, (0, 1, 2, 4, 3, 5))  10.6 us
    convert_element_type x1, other arithmetic, band_table(): return values.astype(jnp.bfloat16)  8.67 us
    reshape x1, local copies, waits for them, and re-layouts, on_device(): jnp.transpose(by_block, (0, 1, 2, 4, 3, 5))  7.79 us

profile of v1, /device:TPU:2, one launch (start us, length us, event | category | flops | bytes accessed | tf_op | source)
XLA Modules:
  0.0 305.7 jit_solution(17131534894433775473)
XLA Ops:
  0.0 0.1 multiply_subtract_fusion
  0.1 0.0 copy-start
  0.1 2.1 fusion.14
  2.2 2.2 fusion.12
  4.4 8.7 %multiply_convert_fusion = bf16[1024,16,128]{2,1,0:T(8,128)(2,1)S(1)} fusion(f32[16,128]{1,0:T(8,128)S(1)} %multiply_subtract_fusion, f32[1024,128]{1,0:T(8,128)S(1)} %get-tuple-element.8, f32[1024,16]{1,0:T(8,128)S(1)} %get-tuple-element.6, f32[1024,128]{1,0:T(8,128)S(1)} %get-tuple-element.7, f32[1024,16]{1,0:T(8,128)S(1)} %get-tuple-element.5), kind=kLoop, calls=%fused_computation | loop fusion | flops 10485760 | bytes 5382144 | tf_op jit(solution)/shard_map/convert_element_type | solution.py:43
  13.1 0.0 copy-done
  13.1 4.5 %multiply_reduce_fusion = (f32[1024]{0:T(1024)S(1)}, f32[1024,1024]{1,0:T(8,128)S(1)}) fusion(bf16[1024,2048]{1,0:T(8,128)(2,1)S(1)} %bitcast.32, bf16[128,8,16,128]{3,2,1,0:T(8,128)(2,1)S(1)} %bitcast.31), kind=kOutput, calls=%fused_computation.6 | convolution fusion | flops 4297063424 | bytes 12587008 | tf_op jit(solution)/shard_map/dot_general | solution.py:128
  17.7 1.9 multiply_convert_fusion.1
  19.6 2.7 reshape.339
  22.4 63.2 %all_to_all.36 = bf16[1,64,4,4,1024]{4,3,2,0,1:T(4,128)(2,1)S(1)} all-to-all(bf16[1,64,4,4,1024]{4,3,2,0,1:T(4,128)(2,1)S(1)} %bitcast.29), channel_id=1, replica_groups=mesh['chan'=64,'tm'=4] {'chan'}, dimensions={1} | all-to-all | bytes 4194304 | tf_op jit(solution)/shard_map/all_to_all | solution.py:134
  85.6 1.2 copy.8
  86.7 31.1 %all_to_all.37 = bf16[64,1,4,4,1024]{4,0,3,1,2:T(8,128)(2,1)S(1)} all-to-all(bf16[64,1,4,4,1024]{4,0,3,1,2:T(8,128)(2,1)S(1)} %copy.8), channel_id=1, replica_groups=mesh['chan'=64,'tm'=4] {'tm'}, dimensions={2} | all-to-all | bytes 4194304 | tf_op jit(solution)/shard_map/all_to_all | solution.py:136
  117.9 3.9 %reshape.340 = bf16[64,4,2,2,16,64]{5,4,0,3,2,1:T(8,128)(2,1)} reshape(bf16[64,1,4,4,1024]{4,0,3,1,2:T(8,128)(2,1)S(1)} %all_to_all.37) | data formatting | bytes 4194304 | tf_op jit(solution)/shard_map/reshape | solution.py:137
  121.8 10.6 %copy.9 = bf16[64,4,2,16,2,64]{5,4,3,2,1,0:T(2,128)(2,1)} copy(bf16[64,4,2,16,2,64]{5,3,0,4,2,1:T(8,128)(2,1)} %bitcast.26) | data formatting | bytes 4194304 | tf_op jit(solution)/shard_map/transpose | solution.py:138
  132.4 7.8 %reshape.341.x_ref = bf16[64,4,32,128]{3,2,1,0:T(8,128)(2,1)} reshape(bf16[64,4,2,16,2,64]{5,4,3,2,1,0:T(2,128)(2,1)} %copy.9) | data formatting | bytes 4194304 | tf_op jit(solution)/shard_map/reshape | solution.py:138
  140.2 46.1 %shard_map.28 = bf16[64,2,2,64,128]{4,3,2,1,0:T(8,128)(2,1)} custom-call(s32[2,64]{1,0:T(2,128)} %pair_ref.1, bf16[64,4,32,128]{3,2,1,0:T(8,128)(2,1)} %reshape.341.x_ref), custom_call_target="tpu_custom_call" | custom-call | tf_op jit(solution)/shard_map/pallas_call | solution.py:88
  186.3 101.8 %all_to_all.38 = bf16[64,256,1,128]{3,1,2,0:T(8,128)(2,1)S(1)} all-to-all(bf16[64,256,1,128]{3,1,2,0:T(8,128)(2,1)} %bitcast.27), channel_id=1, replica_groups=mesh['chan'=64,'tm'=4] {'chan'}, dimensions={0} | all-to-all | bytes 8388608 | tf_op jit(solution)/shard_map/all_to_all | solution.py:144
  288.1 4.6 %copy.20 = bf16[64,256,1,128]{3,0,1,2:T(8,128)(2,1)} copy(bf16[64,256,1,128]{3,1,2,0:T(8,128)(2,1)S(1)} %all_to_all.38) | data formatting | bytes 8388608 | tf_op jit(solution)/shard_map/all_to_all | solution.py:144
  292.7 13.0 %shard_map.29 = bf16[256,64,128]{2,1,0:T(8,128)(2,1)} custom-call(bf16[256,64,128]{2,1,0:T(8,128)(2,1)} %bitcast.28), custom_call_target="tpu_custom_call" | custom-call | tf_op jit(solution)/shard_map/pallas_call | solution.py:112
  (4 shorter events, 0.0 us)
Async XLA Ops:
  0.1 13.0 %copy-start = (bf16[16,64,2048]{2,1,0:T(8,128)(2,1)S(1)}, bf16[16,64,2048]{2,1,0:T(8,128)(2,1)}, u32[]{:S(2)}) copy-start(bf16[16,64,2048]{2,1,0:T(8,128)(2,1)} %param.2) | copy-start | bytes 12582916

commit v2 on v1

--- a/solution.py
+++ b/solution.py
@@ -45,33 +45,34 @@
 
 def pair_kernel(pair_ref, x_ref, o_ref, *, group, day_count, half, width, scale_value):
     step = pl.program_id(0)
-    round_idx = pl.program_id(1)
-    lane = lax.broadcasted_iota(jnp.int32, (width, 2 * width), 1)
-    low_lanes = lane < width
+    rows = 2 * 2 * half
+    row_part = lax.broadcasted_iota(jnp.int32, (rows, 2 * width), 0) // (2 * half)
+    lane_part = lax.broadcasted_iota(jnp.int32, (rows, 2 * width), 1) // width
+    diagonal = row_part == lane_part
+
+    def spread(part):
+        stacked = jnp.concatenate([part, part], axis=0)
+        return jnp.where(diagonal, stacked, jnp.zeros_like(stacked))
 
     def body(k, carry):
         block = step * group + k
-        partner = pair_ref[round_idx, block]
-        acc_re = jnp.zeros((width, 2 * width), jnp.float32)
-        acc_im = jnp.zeros((width, 2 * width), jnp.float32)
+        partners = [pair_ref[r, block] for r in range(ROUNDS)]
+        accs = [jnp.zeros((width, 4 * width), jnp.float32) for _ in range(ROUNDS)]
         for day in range(day_count):
             own = x_ref[block, day]
-            other = x_ref[partner, day]
-            rotated = jnp.concatenate([-other[half:], other[:half]], axis=0)
-            both = jnp.concatenate([other, rotated], axis=1)
-            prods = [
-                lax.dot_general(
-                    own[:, off * width:(off + 1) * width], both,
-                    (((0,), (0,)), ((), ())), preferred_element_type=jnp.float32,
+            lhs = jnp.concatenate([own[:, :width], own[:, width:]], axis=0)
+            for r in range(ROUNDS):
+                other = x_ref[partners[r], day]
+                rotated = jnp.concatenate([-other[half:], other[:half]], axis=0)
+                rhs = jnp.concatenate([spread(other), spread(rotated)], axis=1)
+                prod = lax.dot_general(
+                    lhs, rhs, (((0,), (0,)), ((), ())), preferred_element_type=jnp.float32
                 )
-                for off in range(2)
-            ]
-            re = jnp.where(low_lanes, prods[0][:, :2 * width], prods[1][:, :2 * width])
-            im = jnp.where(low_lanes, prods[0][:, 2 * width:], prods[1][:, 2 * width:])
-            acc_re += (re * scale_value).astype(jnp.bfloat16).astype(jnp.float32)
-            acc_im += (im * scale_value).astype(jnp.bfloat16).astype(jnp.float32)
-        o_ref[k, 0, 0] = acc_re.astype(jnp.bfloat16)
-        o_ref[k, 0, 1] = acc_im.astype(jnp.bfloat16)
+                accs[r] = accs[r] + prod.astype(jnp.bfloat16).astype(jnp.float32)
+        for r in range(ROUNDS):
+            scaled = (accs[r] * scale_value).astype(jnp.bfloat16)
+            o_ref[k, r, 0] = scaled[:, :2 * width]
+            o_ref[k, r, 1] = scaled[:, 2 * width:]
         return carry
 
     lax.fori_loop(0, group, body, 0)
@@ -89,15 +90,14 @@
         kernel,
         grid_spec=pltpu.PrefetchScalarGridSpec(
             num_scalar_prefetch=1,
-            grid=(block_count // group, ROUNDS),
-            in_specs=[pl.BlockSpec(spectra.shape, lambda i, r, pr: (0, 0, 0, 0))],
+            grid=(block_count // group,),
+            in_specs=[pl.BlockSpec(spectra.shape, lambda i, pr: (0, 0, 0, 0))],
             out_specs=pl.BlockSpec(
-                (group, 1, 2, width, lanes), lambda i, r, pr: (i, r, 0, 0, 0)
+                (group, ROUNDS, 2, width, lanes), lambda i, pr: (i, 0, 0, 0, 0)
             ),
         ),
         out_shape=jax.ShapeDtypeStruct((block_count, ROUNDS, 2, width, lanes), jnp.bfloat16),
     )(pairings, spectra)
-
 
 def unshuffle_kernel(x_ref, o_ref, *, group, width):
     for k in range(group):

time: 306 us -> 284 us (0.928)
  Pallas kernels: 59.1 us -> 36.7 us
    pallas_call x1, Pallas kernels: 46.1 us -> 23.8 us  [pair_stage(): pl.pallas_call(kernel, grid_spec=pltpu.PrefetchScalarGridSpec(num_scalar_...]
where the time goes in v2:
time: 284 us; the launch traced here: 283 us
  blocking collectives  196 us (69%)
  Pallas kernels  36.7 us (13%)
  local copies, waits for them, and re-layouts  30.8 us (11%)
  other arithmetic  15 us (5%)
  matrix products  4.54 us (2%)
    all_to_all x1, blocking collectives, on_device(): lax.all_to_all(tiles, 'chan', split_axis=0, concat_axis=2, tiled=True)  102 us
    all_to_all x1, blocking collectives, on_device(): lax.all_to_all(layered, 'chan', split_axis=1, concat_axis=0, tiled=True)  63.2 us
    all_to_all x1, blocking collectives, on_device(): lax.all_to_all(banded, 'tm', split_axis=2, concat_axis=1, tiled=True)  31.1 us
    pallas_call x1, Pallas kernels, pair_stage(): pl.pallas_call(kernel, grid_spec=pltpu.PrefetchScalarGridSpec(num_scalar_...  23.8 us
    pallas_call x1, Pallas kernels, unshuffle_stage(): pl.pallas_call(kernel, grid=(rows // group,), in_specs=[pl.BlockSpec((gro...  13 us
    transpose x1, local copies, waits for them, and re-layouts, on_device(): jnp.transpose(by_block, (0, 1, 2, 4, 3, 5))  10.6 us
    convert_element_type x1, other arithmetic, band_table(): return values.astype(jnp.bfloat16)  8.67 us
    reshape x1, local copies, waits for them, and re-layouts, on_device(): jnp.transpose(by_block, (0, 1, 2, 4, 3, 5))  7.79 us

profile of v2, /device:TPU:2, one launch (start us, length us, event | category | flops | bytes accessed | tf_op | source)
XLA Modules:
  0.0 283.3 jit_solution(1368882382978699665)
XLA Ops:
  0.0 0.1 multiply_subtract_fusion
  0.1 0.0 copy-start
  0.1 2.1 fusion.14
  2.2 2.2 fusion.12
  4.4 8.7 %multiply_convert_fusion = bf16[1024,16,128]{2,1,0:T(8,128)(2,1)S(1)} fusion(f32[16,128]{1,0:T(8,128)S(1)} %multiply_subtract_fusion, f32[1024,128]{1,0:T(8,128)S(1)} %get-tuple-element.8, f32[1024,16]{1,0:T(8,128)S(1)} %get-tuple-element.6, f32[1024,128]{1,0:T(8,128)S(1)} %get-tuple-element.7, f32[1024,16]{1,0:T(8,128)S(1)} %get-tuple-element.5), kind=kLoop, calls=%fused_computation | loop fusion | flops 10485760 | bytes 5382144 | tf_op jit(solution)/shard_map/convert_element_type | solution.py:43
  13.1 0.0 copy-done
  13.1 4.5 %multiply_reduce_fusion = (f32[1024]{0:T(1024)S(1)}, f32[1024,1024]{1,0:T(8,128)S(1)}) fusion(bf16[1024,2048]{1,0:T(8,128)(2,1)S(1)} %bitcast.32, bf16[128,8,16,128]{3,2,1,0:T(8,128)(2,1)S(1)} %bitcast.31), kind=kOutput, calls=%fused_computation.6 | convolution fusion | flops 4297063424 | bytes 12587008 | tf_op jit(solution)/shard_map/dot_general | solution.py:128
  17.7 1.9 multiply_convert_fusion.1
  19.6 2.7 reshape.339
  22.4 63.2 %all_to_all.36 = bf16[1,64,4,4,1024]{4,3,2,0,1:T(4,128)(2,1)S(1)} all-to-all(bf16[1,64,4,4,1024]{4,3,2,0,1:T(4,128)(2,1)S(1)} %bitcast.29), channel_id=1, replica_groups=mesh['chan'=64,'tm'=4] {'chan'}, dimensions={1} | all-to-all | bytes 4194304 | tf_op jit(solution)/shard_map/all_to_all | solution.py:134
  85.6 1.2 copy.8
  86.7 31.1 %all_to_all.37 = bf16[64,1,4,4,1024]{4,0,3,1,2:T(8,128)(2,1)S(1)} all-to-all(bf16[64,1,4,4,1024]{4,0,3,1,2:T(8,128)(2,1)S(1)} %copy.8), channel_id=1, replica_groups=mesh['chan'=64,'tm'=4] {'tm'}, dimensions={2} | all-to-all | bytes 4194304 | tf_op jit(solution)/shard_map/all_to_all | solution.py:136
  117.9 3.9 %reshape.340 = bf16[64,4,2,2,16,64]{5,4,0,3,2,1:T(8,128)(2,1)} reshape(bf16[64,1,4,4,1024]{4,0,3,1,2:T(8,128)(2,1)S(1)} %all_to_all.37) | data formatting | bytes 4194304 | tf_op jit(solution)/shard_map/reshape | solution.py:137
  121.8 10.6 %copy.9 = bf16[64,4,2,16,2,64]{5,4,3,2,1,0:T(2,128)(2,1)} copy(bf16[64,4,2,16,2,64]{5,3,0,4,2,1:T(8,128)(2,1)} %bitcast.26) | data formatting | bytes 4194304 | tf_op jit(solution)/shard_map/transpose | solution.py:138
  132.4 7.8 %reshape.341.x_ref = bf16[64,4,32,128]{3,2,1,0:T(8,128)(2,1)} reshape(bf16[64,4,2,16,2,64]{5,4,3,2,1,0:T(2,128)(2,1)} %copy.9) | data formatting | bytes 4194304 | tf_op jit(solution)/shard_map/reshape | solution.py:138
  140.2 23.8 %shard_map.28 = bf16[64,2,2,64,128]{4,3,2,1,0:T(8,128)(2,1)} custom-call(s32[2,64]{1,0:T(2,128)} %pair_ref.1, bf16[64,4,32,128]{3,2,1,0:T(8,128)(2,1)} %reshape.341.x_ref), custom_call_target="tpu_custom_call" | custom-call | tf_op jit(solution)/shard_map/pallas_call | solution.py:89
  163.9 101.8 %all_to_all.38 = bf16[64,256,1,128]{3,1,2,0:T(8,128)(2,1)S(1)} all-to-all(bf16[64,256,1,128]{3,1,2,0:T(8,128)(2,1)} %bitcast.27), channel_id=1, replica_groups=mesh['chan'=64,'tm'=4] {'chan'}, dimensions={0} | all-to-all | bytes 8388608 | tf_op jit(solution)/shard_map/all_to_all | solution.py:144
  265.7 4.6 %copy.20 = bf16[64,256,1,128]{3,0,1,2:T(8,128)(2,1)} copy(bf16[64,256,1,128]{3,1,2,0:T(8,128)(2,1)S(1)} %all_to_all.38) | data formatting | bytes 8388608 | tf_op jit(solution)/shard_map/all_to_all | solution.py:144
  270.3 13.0 %shard_map.29 = bf16[256,64,128]{2,1,0:T(8,128)(2,1)} custom-call(bf16[256,64,128]{2,1,0:T(8,128)(2,1)} %bitcast.28), custom_call_target="tpu_custom_call" | custom-call | tf_op jit(solution)/shard_map/pallas_call | solution.py:112
  (4 shorter events, 0.0 us)
Async XLA Ops:
  0.1 13.0 %copy-start = (bf16[16,64,2048]{2,1,0:T(8,128)(2,1)S(1)}, bf16[16,64,2048]{2,1,0:T(8,128)(2,1)}, u32[]{:S(2)}) copy-start(bf16[16,64,2048]{2,1,0:T(8,128)(2,1)} %param.2) | copy-start | bytes 12582916

commit v3 on v2

--- a/solution.py
+++ b/solution.py
@@ -130,10 +130,9 @@
     )
     power_sum = jnp.sum(spectra * spectra, axis=0) / F
     whitened = (spectra * lax.rsqrt(power_sum + 1e-06)[None, :]).astype(jnp.bfloat16)
-    layered = whitened.reshape(1, chan_count, day_count, 2 * per_piece, win_count * block_width)
-    banded = lax.all_to_all(layered, "chan", split_axis=1, concat_axis=0, tiled=True)
+    layered = whitened.reshape(chan_count * day_count, 2 * per_piece, win_count * block_width)
     scale_value = 1.0 / math.sqrt(win_count * day_count)
-    pooled = lax.all_to_all(banded, "tm", split_axis=2, concat_axis=1, tiled=True)
+    pooled = lax.all_to_all(layered, ("chan", "tm"), split_axis=0, concat_axis=0, tiled=True)
     by_block = pooled.reshape(chan_count, day_count, 2, per_piece, win_count, block_width)
     by_block = jnp.transpose(by_block, (0, 1, 2, 4, 3, 5)).reshape(
         chan_count, day_count, 2 * win_count, per_piece * block_width

time: 284 us -> 258 us (0.908)
  blocking collectives: 196 us -> 169 us
    all_to_all x2 -> x1, blocking collectives: 94.4 us -> 66.6 us  [on_device(): lax.all_to_all(layered, ('chan', 'tm'), split_axis=0, concat_axis=0, tile...]
where the time goes in v3:
time: 258 us; the launch traced here: 257 us
  blocking collectives  169 us (66%)
  Pallas kernels  36.7 us (14%)
  local copies, waits for them, and re-layouts  31.6 us (12%)
  other arithmetic  15 us (6%)
  matrix products  4.54 us (2%)
    all_to_all x1, blocking collectives, on_device(): lax.all_to_all(tiles, 'chan', split_axis=0, concat_axis=2, tiled=True)  102 us
    all_to_all x1, blocking collectives, on_device(): lax.all_to_all(layered, ('chan', 'tm'), split_axis=0, concat_axis=0, tile...  66.6 us
    pallas_call x1, Pallas kernels, pair_stage(): pl.pallas_call(kernel, grid_spec=pltpu.PrefetchScalarGridSpec(num_scalar_...  23.8 us
    pallas_call x1, Pallas kernels, unshuffle_stage(): pl.pallas_call(kernel, grid=(rows // group,), in_specs=[pl.BlockSpec((gro...  13 us
    transpose x1, local copies, waits for them, and re-layouts, on_device(): jnp.transpose(by_block, (0, 1, 2, 4, 3, 5))  11.9 us
    convert_element_type x1, other arithmetic, band_table(): return values.astype(jnp.bfloat16)  8.67 us
    reshape x1, local copies, waits for them, and re-layouts, on_device(): jnp.transpose(by_block, (0, 1, 2, 4, 3, 5))  7.79 us

profile of v3, /device:TPU:2, one launch (start us, length us, event | category | flops | bytes accessed | tf_op | source)
XLA Modules:
  0.0 257.0 jit_solution(367194324280557041)
XLA Ops:
  0.0 0.1 multiply_subtract_fusion
  0.1 0.0 copy-start
  0.1 2.1 fusion.14
  2.2 2.2 fusion.12
  4.4 8.7 %multiply_convert_fusion = bf16[1024,16,128]{2,1,0:T(8,128)(2,1)S(1)} fusion(f32[16,128]{1,0:T(8,128)S(1)} %multiply_subtract_fusion, f32[1024,128]{1,0:T(8,128)S(1)} %get-tuple-element.8, f32[1024,16]{1,0:T(8,128)S(1)} %get-tuple-element.6, f32[1024,128]{1,0:T(8,128)S(1)} %get-tuple-element.7, f32[1024,16]{1,0:T(8,128)S(1)} %get-tuple-element.5), kind=kLoop, calls=%fused_computation | loop fusion | flops 10485760 | bytes 5382144 | tf_op jit(solution)/shard_map/convert_element_type | solution.py:43
  13.1 0.0 copy-done
  13.1 4.5 %multiply_reduce_fusion = (f32[1024]{0:T(1024)S(1)}, f32[1024,1024]{1,0:T(8,128)S(1)}) fusion(bf16[1024,2048]{1,0:T(8,128)(2,1)S(1)} %bitcast.26, bf16[128,8,16,128]{3,2,1,0:T(8,128)(2,1)S(1)} %bitcast.25), kind=kOutput, calls=%fused_computation.6 | convolution fusion | flops 4297063424 | bytes 12587008 | tf_op jit(solution)/shard_map/dot_general | solution.py:128
  17.7 1.9 multiply_convert_fusion.1
  19.6 2.7 %reshape.332 = bf16[256,4,1024]{2,1,0:T(4,128)(2,1)S(1)} reshape(bf16[1024,1024]{1,0:T(8,128)(2,1)} %multiply_convert_fusion.1) | data formatting | bytes 4194304 | tf_op jit(solution)/shard_map/reshape | solution.py:133
  22.4 66.6 %all_to_all.20 = bf16[256,4,1024]{2,1,0:T(4,128)(2,1)S(1)} all-to-all(bf16[256,4,1024]{2,1,0:T(4,128)(2,1)S(1)} %reshape.332), channel_id=1, replica_groups=mesh['chan'=64,'tm'=4] {'chan','tm'}, dimensions={0} | all-to-all | bytes 4194304 | tf_op jit(solution)/shard_map/all_to_all | solution.py:135
  88.9 0.6 copy.7
  89.6 3.9 %reshape.333 = bf16[64,4,2,2,16,64]{5,4,1,0,3,2:T(8,128)(2,1)} reshape(bf16[256,4,1024]{2,0,1:T(8,128)(2,1)S(1)} %copy.7) | data formatting | bytes 4194304 | tf_op jit(solution)/shard_map/reshape | solution.py:136
  93.5 11.9 %copy.8 = bf16[64,4,2,16,2,64]{5,4,3,2,1,0:T(2,128)(2,1)} copy(bf16[64,4,2,16,2,64]{5,3,1,0,4,2:T(8,128)(2,1)} %bitcast.22) | data formatting | bytes 4194304 | tf_op jit(solution)/shard_map/transpose | solution.py:137
  105.4 7.8 %reshape.334.x_ref = bf16[64,4,32,128]{3,2,1,0:T(8,128)(2,1)} reshape(bf16[64,4,2,16,2,64]{5,4,3,2,1,0:T(2,128)(2,1)} %copy.8) | data formatting | bytes 4194304 | tf_op jit(solution)/shard_map/reshape | solution.py:137
  113.2 23.8 %shard_map.28 = bf16[64,2,2,64,128]{4,3,2,1,0:T(8,128)(2,1)} custom-call(s32[2,64]{1,0:T(2,128)} %pair_ref.1, bf16[64,4,32,128]{3,2,1,0:T(8,128)(2,1)} %reshape.334.x_ref), custom_call_target="tpu_custom_call" | custom-call | tf_op jit(solution)/shard_map/pallas_call | solution.py:89
  136.9 102.4 %all_to_all.21 = bf16[64,256,1,128]{3,1,2,0:T(8,128)(2,1)S(1)} all-to-all(bf16[64,256,1,128]{3,1,2,0:T(8,128)(2,1)} %bitcast.23), channel_id=1, replica_groups=mesh['chan'=64,'tm'=4] {'chan'}, dimensions={0} | all-to-all | bytes 8388608 | tf_op jit(solution)/shard_map/all_to_all | solution.py:143
  239.4 4.6 %copy.19 = bf16[64,256,1,128]{3,0,1,2:T(8,128)(2,1)} copy(bf16[64,256,1,128]{3,1,2,0:T(8,128)(2,1)S(1)} %all_to_all.21) | data formatting | bytes 8388608 | tf_op jit(solution)/shard_map/all_to_all | solution.py:143
  244.0 13.0 %shard_map.29 = bf16[256,64,128]{2,1,0:T(8,128)(2,1)} custom-call(bf16[256,64,128]{2,1,0:T(8,128)(2,1)} %bitcast.24), custom_call_target="tpu_custom_call" | custom-call | tf_op jit(solution)/shard_map/pallas_call | solution.py:112
  (4 shorter events, 0.0 us)
Async XLA Ops:
  0.1 13.0 %copy-start = (bf16[16,64,2048]{2,1,0:T(8,128)(2,1)S(1)}, bf16[16,64,2048]{2,1,0:T(8,128)(2,1)}, u32[]{:S(2)}) copy-start(bf16[16,64,2048]{2,1,0:T(8,128)(2,1)} %param.2) | copy-start | bytes 12582916

commit v4 on v3

--- a/solution.py
+++ b/solution.py
@@ -43,7 +43,7 @@
     return values.astype(jnp.bfloat16)
 
 
-def pair_kernel(pair_ref, x_ref, o_ref, *, group, day_count, half, width, scale_value):
+def pair_kernel(pair_ref, x_ref, o_ref, *, group, day_count, half, width, scale_value, rounds):
     step = pl.program_id(0)
     rows = 2 * 2 * half
     row_part = lax.broadcasted_iota(jnp.int32, (rows, 2 * width), 0) // (2 * half)
@@ -56,12 +56,12 @@
 
     def body(k, carry):
         block = step * group + k
-        partners = [pair_ref[r, block] for r in range(ROUNDS)]
-        accs = [jnp.zeros((width, 4 * width), jnp.float32) for _ in range(ROUNDS)]
+        partners = [pair_ref[r, block] for r in rounds]
+        accs = [jnp.zeros((width, 4 * width), jnp.float32) for _ in rounds]
         for day in range(day_count):
             own = x_ref[block, day]
             lhs = jnp.concatenate([own[:, :width], own[:, width:]], axis=0)
-            for r in range(ROUNDS):
+            for r in range(len(rounds)):
                 other = x_ref[partners[r], day]
                 rotated = jnp.concatenate([-other[half:], other[:half]], axis=0)
                 rhs = jnp.concatenate([spread(other), spread(rotated)], axis=1)
@@ -69,7 +69,7 @@
                     lhs, rhs, (((0,), (0,)), ((), ())), preferred_element_type=jnp.float32
                 )
                 accs[r] = accs[r] + prod.astype(jnp.bfloat16).astype(jnp.float32)
-        for r in range(ROUNDS):
+        for r in range(len(rounds)):
             scaled = (accs[r] * scale_value).astype(jnp.bfloat16)
             o_ref[k, r, 0] = scaled[:, :2 * width]
             o_ref[k, r, 1] = scaled[:, 2 * width:]
@@ -78,13 +78,13 @@
     lax.fori_loop(0, group, body, 0)
 
 
-def pair_stage(pairings, spectra, scale_value):
+def pair_stage(pairings, spectra, scale_value, rounds=tuple(range(ROUNDS))):
     block_count, day_count, rows, lanes = spectra.shape
     width = lanes // 2
     group = 8
     kernel = functools.partial(
         pair_kernel, group=group, day_count=day_count, half=rows // 2, width=width,
-        scale_value=scale_value,
+        scale_value=scale_value, rounds=rounds,
     )
     return pl.pallas_call(
         kernel,
@@ -93,10 +93,10 @@
             grid=(block_count // group,),
             in_specs=[pl.BlockSpec(spectra.shape, lambda i, pr: (0, 0, 0, 0))],
             out_specs=pl.BlockSpec(
-                (group, ROUNDS, 2, width, lanes), lambda i, pr: (i, 0, 0, 0, 0)
+                (group, len(rounds), 2, width, lanes), lambda i, pr: (i, 0, 0, 0, 0)
             ),
         ),
-        out_shape=jax.ShapeDtypeStruct((block_count, ROUNDS, 2, width, lanes), jnp.bfloat16),
+        out_shape=jax.ShapeDtypeStruct((block_count, len(rounds), 2, width, lanes), jnp.bfloat16),
     )(pairings, spectra)
 
 def unshuffle_kernel(x_ref, o_ref, *, group, width):
@@ -137,11 +137,14 @@
     by_block = jnp.transpose(by_block, (0, 1, 2, 4, 3, 5)).reshape(
         chan_count, day_count, 2 * win_count, per_piece * block_width
     )
-    tiles = pair_stage(pairings, by_block, scale_value)
-    rows = ROUNDS * 2 * block_width
-    tiles = tiles.reshape(chan_count, rows, 1, 2 * block_width)
-    received = lax.all_to_all(tiles, "chan", split_axis=0, concat_axis=2, tiled=True)
-    stacked = unshuffle_stage(received.reshape(rows, chan_count, 2 * block_width))
+    rows = 2 * block_width
+    parts = []
+    for round_idx in range(ROUNDS):
+        tiles = pair_stage(pairings, by_block, scale_value, (round_idx,))
+        tiles = tiles.reshape(chan_count, rows, 1, 2 * block_width)
+        received = lax.all_to_all(tiles, "chan", split_axis=0, concat_axis=2, tiled=True)
+        parts.append(unshuffle_stage(received.reshape(rows, chan_count, 2 * block_width)))
+    stacked = jnp.stack(parts)
     return stacked.reshape(ROUNDS, 2, block_width, block_width, per_piece * chan_count)
 
 def solution(mesh):

time: 258 us -> 265 us (1.027)
  blocking collectives: 169 us -> 66.6 us
  waiting for transfers between devices: 0 us -> 69 us
  Pallas kernels: 36.7 us -> 56.3 us
  starting transfers between devices: 0 us -> 13.9 us
  other arithmetic: 15 us -> 19 us
    all_to_all x1 -> x0, blocking collectives: 102 us -> none  [on_device(): lax.all_to_all(tiles, 'chan', split_axis=0, concat_axis=2, tiled=True)]
    all_to_all x0 -> x2, waiting for transfers between devices: none -> 69 us  [on_device(): lax.all_to_all(tiles, 'chan', split_axis=0, concat_axis=2, tiled=True)]
    pallas_call x1 -> x2, Pallas kernels: 23.8 us -> 42.2 us  [pair_stage(): pl.pallas_call(kernel, grid_spec=pltpu.PrefetchScalarGridSpec(num_scalar_...]
    all_to_all x0 -> x2, starting transfers between devices: none -> 13.9 us  [on_device(): lax.all_to_all(tiles, 'chan', split_axis=0, concat_axis=2, tiled=True)]
    another operation x0 -> x1, other arithmetic: none -> 3.99 us  [on_device(): stacked = jnp.stack(parts)]
    all_to_all x1 -> x2, local copies, waits for them, and re-layouts: 4.63 us -> 6.93 us  [on_device(): lax.all_to_all(tiles, 'chan', split_axis=0, concat_axis=2, tiled=True)]
    pallas_call x1 -> x2, Pallas kernels: 13 us -> 14.1 us  [unshuffle_stage(): pl.pallas_call(kernel, grid=(rows // group,), in_specs=[pl.BlockSpec((gro...]
  transfers between devices with their start and end apart: 0 -> 2, of which waited for: 0 -> 2; matrix products, arithmetic and copies ran while one was open for 0% -> 1% of each run, Pallas kernels for 0% -> 11%
where the time goes in v4:
time: 265 us; the launch traced here: 263 us
  waiting for transfers between devices  69 us (26%)
  blocking collectives  66.6 us (25%)
  Pallas kernels  56.3 us (21%)
  local copies, waits for them, and re-layouts  33.9 us (13%)
  other arithmetic  19 us (7%)
  starting transfers between devices  13.9 us (5%)
  matrix products  4.54 us (2%)
    all_to_all x2, waiting for transfers between devices, on_device(): lax.all_to_all(tiles, 'chan', split_axis=0, concat_axis=2, tiled=True)  69 us
    all_to_all x1, blocking collectives, on_device(): lax.all_to_all(layered, ('chan', 'tm'), split_axis=0, concat_axis=0, tile...  66.6 us
    pallas_call x2, Pallas kernels, pair_stage(): pl.pallas_call(kernel, grid_spec=pltpu.PrefetchScalarGridSpec(num_scalar_...  42.2 us
    pallas_call x2, Pallas kernels, unshuffle_stage(): pl.pallas_call(kernel, grid=(rows // group,), in_specs=[pl.BlockSpec((gro...  14.1 us
    all_to_all x2, starting transfers between devices, on_device(): lax.all_to_all(tiles, 'chan', split_axis=0, concat_axis=2, tiled=True)  13.9 us
    transpose x1, local copies, waits for them, and re-layouts, on_device(): jnp.transpose(by_block, (0, 1, 2, 4, 3, 5))  11.9 us
    convert_element_type x1, other arithmetic, band_table(): return values.astype(jnp.bfloat16)  8.67 us
    reshape x1, local copies, waits for them, and re-layouts, on_device(): jnp.transpose(by_block, (0, 1, 2, 4, 3, 5))  7.78 us
  transfers between devices with their start and end apart: 2, of which 2 were waited for; matrix products, arithmetic and copies ran while one was open for 1% of the time, Pallas kernels for 11%

profile of v4, /device:TPU:2, one launch (start us, length us, event | category | flops | bytes accessed | tf_op | source)
XLA Modules:
  0.0 263.3 jit_solution(582545518550917313)
XLA Ops:
  0.0 0.1 multiply_subtract_fusion
  0.1 0.0 copy-start.1
  0.1 2.1 fusion.14
  2.2 2.2 fusion.12
  4.4 8.7 %multiply_convert_fusion = bf16[1024,16,128]{2,1,0:T(8,128)(2,1)S(1)} fusion(f32[16,128]{1,0:T(8,128)S(1)} %multiply_subtract_fusion, f32[1024,128]{1,0:T(8,128)S(1)} %get-tuple-element.8, f32[1024,16]{1,0:T(8,128)S(1)} %get-tuple-element.6, f32[1024,128]{1,0:T(8,128)S(1)} %get-tuple-element.7, f32[1024,16]{1,0:T(8,128)S(1)} %get-tuple-element.5), kind=kLoop, calls=%fused_computation | loop fusion | flops 10485760 | bytes 5382144 | tf_op jit(solution)/shard_map/convert_element_type | solution.py:43
  13.1 0.0 copy-done.1
  13.1 4.5 %multiply_reduce_fusion = (f32[1024]{0:T(1024)S(1)}, f32[1024,1024]{1,0:T(8,128)S(1)}) fusion(bf16[1024,2048]{1,0:T(8,128)(2,1)S(1)} %bitcast.41, bf16[128,8,16,128]{3,2,1,0:T(8,128)(2,1)S(1)} %bitcast.40), kind=kOutput, calls=%fused_computation.6 | convolution fusion | flops 4297063424 | bytes 12587008 | tf_op jit(solution)/shard_map/dot_general | solution.py:128
  17.7 1.9 multiply_convert_fusion.1
  19.6 2.7 %reshape.341 = bf16[256,4,1024]{2,1,0:T(4,128)(2,1)S(1)} reshape(bf16[1024,1024]{1,0:T(8,128)(2,1)} %multiply_convert_fusion.1) | data formatting | bytes 4194304 | tf_op jit(solution)/shard_map/reshape | solution.py:133
  22.4 66.6 %all_to_all.35 = bf16[256,4,1024]{2,1,0:T(4,128)(2,1)S(1)} all-to-all(bf16[256,4,1024]{2,1,0:T(4,128)(2,1)S(1)} %reshape.341), channel_id=1, replica_groups=mesh['chan'=64,'tm'=4] {'chan','tm'}, dimensions={0} | all-to-all | bytes 4194304 | tf_op jit(solution)/shard_map/all_to_all | solution.py:135
  88.9 0.6 copy.9
  89.6 3.9 %reshape.342 = bf16[64,4,2,2,16,64]{5,4,1,0,3,2:T(8,128)(2,1)} reshape(bf16[256,4,1024]{2,0,1:T(8,128)(2,1)S(1)} %copy.9) | data formatting | bytes 4194304 | tf_op jit(solution)/shard_map/reshape | solution.py:136
  93.5 11.9 %copy.10 = bf16[64,4,2,16,2,64]{5,4,3,2,1,0:T(2,128)(2,1)} copy(bf16[64,4,2,16,2,64]{5,3,1,0,4,2:T(8,128)(2,1)} %bitcast.33) | data formatting | bytes 4194304 | tf_op jit(solution)/shard_map/transpose | solution.py:137
  105.4 7.8 %reshape.343.x_ref = bf16[64,4,32,128]{3,2,1,0:T(8,128)(2,1)} reshape(bf16[64,4,2,16,2,64]{5,4,3,2,1,0:T(2,128)(2,1)} %copy.10) | data formatting | bytes 4194304 | tf_op jit(solution)/shard_map/reshape | solution.py:137
  113.2 21.1 %shard_map.30 = bf16[64,1,2,64,128]{4,3,2,1,0:T(8,128)(2,1)} custom-call(s32[2,64]{1,0:T(2,128)} %pair_ref.3, bf16[64,4,32,128]{3,2,1,0:T(8,128)(2,1)} %reshape.343.x_ref), custom_call_target="tpu_custom_call" | custom-call | tf_op jit(solution)/shard_map/pallas_call | solution.py:89
  134.3 6.9 %all-to-all-start.2 = ((bf16[64,128,1,128]{3,1,2,0:T(8,128)(2,1)}), bf16[64,128,1,128]{3,1,2,0:T(8,128)(2,1)S(1)}, u32[]{:S(2)}, u32[]{:S(2)}) async-start(bf16[64,128,1,128]{3,1,2,0:T(8,128)(2,1)} %bitcast.35), calls=%async_computation.2 | async-start | bytes 4194304 | tf_op jit(solution)/shard_map/all_to_all | solution.py:145
  141.1 21.1 %shard_map.28 = bf16[64,1,2,64,128]{4,3,2,1,0:T(8,128)(2,1)} custom-call(s32[2,64]{1,0:T(2,128)} %pair_ref.3, bf16[64,4,32,128]{3,2,1,0:T(8,128)(2,1)} %reshape.343.x_ref), custom_call_target="tpu_custom_call" | custom-call | tf_op jit(solution)/shard_map/pallas_call | solution.py:89
  162.3 29.5 %all-to-all-done.2 = bf16[64,128,1,128]{3,1,2,0:T(8,128)(2,1)S(1)} async-done(((bf16[64,128,1,128]{3,1,2,0:T(8,128)(2,1)}), bf16[64,128,1,128]{3,1,2,0:T(8,128)(2,1)S(1)}, u32[]{:S(2)}, u32[]{:S(2)}) %all-to-all-start.2) | async-done | bytes 2097184 | tf_op jit(solution)/shard_map/all_to_all | solution.py:145
  191.8 7.0 %all-to-all-start.1 = ((bf16[64,128,1,128]{3,1,2,0:T(8,128)(2,1)}), bf16[64,128,1,128]{3,1,2,0:T(8,128)(2,1)}, u32[]{:S(2)}, u32[]{:S(2)}) async-start(bf16[64,128,1,128]{3,1,2,0:T(8,128)(2,1)} %bitcast.34), calls=%async_computation.1 | async-start | bytes 4194304 | tf_op jit(solution)/shard_map/all_to_all | solution.py:145
  198.8 2.7 %copy.24 = bf16[64,128,1,128]{3,0,1,2:T(8,128)(2,1)} copy(bf16[64,128,1,128]{3,1,2,0:T(8,128)(2,1)S(1)} %all-to-all-done.2) | data formatting | bytes 4194304 | tf_op jit(solution)/shard_map/all_to_all | solution.py:145
  201.5 7.1 %shard_map.31 = bf16[128,64,128]{2,1,0:T(8,128)(2,1)} custom-call(bf16[128,64,128]{2,1,0:T(8,128)(2,1)} %bitcast.36), custom_call_target="tpu_custom_call" | custom-call | tf_op jit(solution)/shard_map/pallas_call | solution.py:112
  208.5 0.0 copy-start
  208.5 39.5 %all-to-all-done.1 = bf16[64,128,1,128]{3,1,2,0:T(8,128)(2,1)} async-done(((bf16[64,128,1,128]{3,1,2,0:T(8,128)(2,1)}), bf16[64,128,1,128]{3,1,2,0:T(8,128)(2,1)}, u32[]{:S(2)}, u32[]{:S(2)}) %all-to-all-start.1) | async-done | bytes 2097184 | tf_op jit(solution)/shard_map/all_to_all | solution.py:145
  248.0 4.3 %copy.25 = bf16[64,128,1,128]{3,0,1,2:T(8,128)(2,1)} copy(bf16[64,128,1,128]{3,1,2,0:T(8,128)(2,1)} %all-to-all-done.1) | data formatting | bytes 4194304 | tf_op jit(solution)/shard_map/all_to_all | solution.py:145
  252.3 7.0 %shard_map.29 = bf16[128,64,128]{2,1,0:T(8,128)(2,1)} custom-call(bf16[128,64,128]{2,1,0:T(8,128)(2,1)} %bitcast.37), custom_call_target="tpu_custom_call" | custom-call | tf_op jit(solution)/shard_map/pallas_call | solution.py:112
  259.3 0.0 copy-done
  259.3 4.0 %pad_maximum_fusion = bf16[2,2,64,64,128]{4,3,2,1,0:T(8,128)(2,1)} fusion(bf16[1,2,64,64,128]{4,3,2,1,0:T(8,128)(2,1)S(1)} %bitcast.38, bf16[1,2,64,64,128]{4,3,2,1,0:T(8,128)(2,1)} %bitcast.39), kind=kLoop, calls=%fused_computation.4 | loop fusion | flops 2097152 | bytes 8388608 | tf_op jit(solution)/shard_map/stack | solution.py:147
  (4 shorter events, 0.0 us)
Async XLA Ops:
  0.1 13.0 %copy-start.1 = (bf16[16,64,2048]{2,1,0:T(8,128)(2,1)S(1)}, bf16[16,64,2048]{2,1,0:T(8,128)(2,1)}, u32[]{:S(2)}) copy-start(bf16[16,64,2048]{2,1,0:T(8,128)(2,1)} %param.2) | copy-start | bytes 12582916
  134.3 57.5 %all-to-all-start.2 = ((bf16[64,128,1,128]{3,1,2,0:T(8,128)(2,1)}), bf16[64,128,1,128]{3,1,2,0:T(8,128)(2,1)S(1)}, u32[]{:S(2)}, u32[]{:S(2)}) async-start(bf16[64,128,1,128]{3,1,2,0:T(8,128)(2,1)} %bitcast.35), calls=%async_computation.2 | async-start | bytes 4194304 | tf_op jit(solution)/shard_map/all_to_all | solution.py:145
  191.8 56.2 %all-to-all-start.1 = ((bf16[64,128,1,128]{3,1,2,0:T(8,128)(2,1)}), bf16[64,128,1,128]{3,1,2,0:T(8,128)(2,1)}, u32[]{:S(2)}, u32[]{:S(2)}) async-start(bf16[64,128,1,128]{3,1,2,0:T(8,128)(2,1)} %bitcast.34), calls=%async_computation.1 | async-start | bytes 4194304 | tf_op jit(solution)/shard_map/all_to_all | solution.py:145
  208.5 50.8 %copy-start = (bf16[128,64,128]{2,1,0:T(8,128)(2,1)S(1)}, bf16[128,64,128]{2,1,0:T(8,128)(2,1)}, u32[]{:S(2)}) copy-start(bf16[128,64,128]{2,1,0:T(8,128)(2,1)} %shard_map.31) | copy-start | bytes 6291460

commit v5 on v3

--- a/solution.py
+++ b/solution.py
@@ -2,6 +2,8 @@
 import math
 
 import jax
+import ml_dtypes
+import numpy as np
 import jax.numpy as jnp
 from jax import lax
 from jax.experimental import pallas as pl
@@ -15,7 +17,7 @@
 
 def band_table(chan_count, day_count):
     per_piece = F // (chan_count * day_count)
-    row_ids = jnp.arange(2 * F, dtype=jnp.int32)
+    row_ids = np.arange(2 * F, dtype=np.int64)
     piece_idx = row_ids // (day_count * 2 * per_piece)
     remainder = row_ids % (day_count * 2 * per_piece)
     group_idx = remainder // (2 * per_piece)
@@ -23,25 +25,11 @@
     imag_flag = within // per_piece
     offset_idx = within % per_piece
     freq_ids = group_idx * (chan_count * per_piece) + offset_idx * chan_count + piece_idx
-    lanes = 128
-    hi_ids = jnp.arange(L // lanes, dtype=jnp.int32)
-    lo_ids = jnp.arange(lanes, dtype=jnp.int32)
-    two_pi = 2.0 * math.pi / L
-    hi_angle = ((freq_ids[:, None] + 1) * (hi_ids[None, :] * lanes) % L).astype(jnp.float32) * two_pi
-    lo_angle = ((freq_ids[:, None] + 1) * lo_ids[None, :] % L).astype(jnp.float32) * two_pi
-    hi_cos, hi_sin = jnp.cos(hi_angle), jnp.sin(hi_angle)
-    lo_cos, lo_sin = jnp.cos(lo_angle), jnp.sin(lo_angle)
-    is_real = (imag_flag == 0)[:, None]
-    first = jnp.where(is_real, hi_cos, -hi_sin)
-    second = jnp.where(is_real, -hi_sin, -hi_cos)
-    samples = jnp.arange(L, dtype=jnp.int32).reshape(L // lanes, lanes)
-    taper_vals = 0.5 - 0.5 * jnp.cos((samples.astype(jnp.float32) + 0.5) * (2.0 * math.pi / L))
-    values = (
-        first[:, :, None] * lo_cos[:, None, :] + second[:, :, None] * lo_sin[:, None, :]
-    ) * taper_vals[None]
-    values = values.reshape(2 * F, L)
-    return values.astype(jnp.bfloat16)
-
+    samples = np.arange(L, dtype=np.int64)
+    angles = ((freq_ids[:, None] + 1) * samples[None, :] % L) * (2.0 * np.pi / L)
+    taper_vals = 0.5 - 0.5 * np.cos((samples + 0.5) * (2.0 * np.pi / L))
+    values = np.where(imag_flag[:, None] == 0, np.cos(angles), -np.sin(angles)) * taper_vals[None]
+    return jnp.asarray(values.astype(ml_dtypes.bfloat16))
 
 def pair_kernel(pair_ref, x_ref, o_ref, *, group, day_count, half, width, scale_value):
     step = pl.program_id(0)

time: 258 us -> 248 us (0.961)
  other arithmetic: 15 us -> 1.94 us
  matrix products: 4.54 us -> 7.61 us
    convert_element_type x1 -> x0, other arithmetic: 8.67 us -> none  [band_table(): return values.astype(jnp.bfloat16)]
    dot_general x1, matrix products: 4.54 us -> 7.61 us  [on_device(): lax.dot_general(dft_table, flat_raw, (((1,), (1,)), ((), ())), preferred_...]
where the time goes in v5:
time: 248 us; the launch traced here: 247 us
  blocking collectives  169 us (68%)
  Pallas kernels  36.7 us (15%)
  local copies, waits for them, and re-layouts  31.6 us (13%)
  matrix products  7.61 us (3%)
    all_to_all x1, blocking collectives, on_device(): lax.all_to_all(tiles, 'chan', split_axis=0, concat_axis=2, tiled=True)  102 us
    all_to_all x1, blocking collectives, on_device(): lax.all_to_all(layered, ('chan', 'tm'), split_axis=0, concat_axis=0, tile...  66.6 us
    pallas_call x1, Pallas kernels, pair_stage(): pl.pallas_call(kernel, grid_spec=pltpu.PrefetchScalarGridSpec(num_scalar_...  23.8 us
    pallas_call x1, Pallas kernels, unshuffle_stage(): pl.pallas_call(kernel, grid=(rows // group,), in_specs=[pl.BlockSpec((gro...  13 us
    transpose x1, local copies, waits for them, and re-layouts, on_device(): jnp.transpose(by_block, (0, 1, 2, 4, 3, 5))  11.9 us
    reshape x1, local copies, waits for them, and re-layouts, on_device(): jnp.transpose(by_block, (0, 1, 2, 4, 3, 5))  7.79 us
    dot_general x1, matrix products, on_device(): lax.dot_general(dft_table, flat_raw, (((1,), (1,)), ((), ())), preferred_...  7.61 us

profile of v5, /device:TPU:2, one launch (start us, length us, event | category | flops | bytes accessed | tf_op | source)
XLA Modules:
  0.0 246.9 jit_solution(16399908502133608940)
XLA Ops:
  0.0 7.6 %multiply_reduce_fusion = (f32[1024]{0:T(1024)S(1)}, f32[1024,1024]{1,0:T(8,128)S(1)}) fusion(bf16[1024,2048]{1,0:T(8,128)(2,1)} %constant.9.clone, bf16[1024,2048]{1,0:T(8,128)(2,1)} %bitcast.20), kind=kOutput, calls=%fused_computation.2 | convolution fusion | flops 4297063424 | bytes 12587008 | tf_op jit(solution)/shard_map/dot_general | solution.py:116
  7.6 1.9 multiply_convert_fusion
  9.6 2.7 %reshape.28 = bf16[256,4,1024]{2,1,0:T(4,128)(2,1)S(1)} reshape(bf16[1024,1024]{1,0:T(8,128)(2,1)} %multiply_convert_fusion) | data formatting | bytes 4194304 | tf_op jit(solution)/shard_map/reshape | solution.py:121
  12.3 66.6 %all_to_all.20 = bf16[256,4,1024]{2,1,0:T(4,128)(2,1)S(1)} all-to-all(bf16[256,4,1024]{2,1,0:T(4,128)(2,1)S(1)} %reshape.28), channel_id=1, replica_groups=mesh['chan'=64,'tm'=4] {'chan','tm'}, dimensions={0} | all-to-all | bytes 4194304 | tf_op jit(solution)/shard_map/all_to_all | solution.py:123
  78.9 0.6 copy.8
  79.5 3.9 %reshape.29 = bf16[64,4,2,2,16,64]{5,4,1,0,3,2:T(8,128)(2,1)} reshape(bf16[256,4,1024]{2,0,1:T(8,128)(2,1)S(1)} %copy.8) | data formatting | bytes 4194304 | tf_op jit(solution)/shard_map/reshape | solution.py:124
  83.5 11.9 %copy.9 = bf16[64,4,2,16,2,64]{5,4,3,2,1,0:T(2,128)(2,1)} copy(bf16[64,4,2,16,2,64]{5,3,1,0,4,2:T(8,128)(2,1)} %bitcast.17) | data formatting | bytes 4194304 | tf_op jit(solution)/shard_map/transpose | solution.py:125
  95.3 7.8 %reshape.30.x_ref = bf16[64,4,32,128]{3,2,1,0:T(8,128)(2,1)} reshape(bf16[64,4,2,16,2,64]{5,4,3,2,1,0:T(2,128)(2,1)} %copy.9) | data formatting | bytes 4194304 | tf_op jit(solution)/shard_map/reshape | solution.py:125
  103.1 23.8 %shard_map.37 = bf16[64,2,2,64,128]{4,3,2,1,0:T(8,128)(2,1)} custom-call(s32[2,64]{1,0:T(2,128)} %pair_ref.1, bf16[64,4,32,128]{3,2,1,0:T(8,128)(2,1)} %reshape.30.x_ref), custom_call_target="tpu_custom_call" | custom-call | tf_op jit(solution)/shard_map/pallas_call | solution.py:77
  126.9 102.4 %all_to_all.21 = bf16[64,256,1,128]{3,1,2,0:T(8,128)(2,1)S(1)} all-to-all(bf16[64,256,1,128]{3,1,2,0:T(8,128)(2,1)} %bitcast.18), channel_id=1, replica_groups=mesh['chan'=64,'tm'=4] {'chan'}, dimensions={0} | all-to-all | bytes 8388608 | tf_op jit(solution)/shard_map/all_to_all | solution.py:131
  229.3 4.6 %copy.13 = bf16[64,256,1,128]{3,0,1,2:T(8,128)(2,1)} copy(bf16[64,256,1,128]{3,1,2,0:T(8,128)(2,1)S(1)} %all_to_all.21) | data formatting | bytes 8388608 | tf_op jit(solution)/shard_map/all_to_all | solution.py:131
  233.9 13.0 %shard_map.38 = bf16[256,64,128]{2,1,0:T(8,128)(2,1)} custom-call(bf16[256,64,128]{2,1,0:T(8,128)(2,1)} %bitcast.19), custom_call_target="tpu_custom_call" | custom-call | tf_op jit(solution)/shard_map/pallas_call | solution.py:100
  (1 shorter events, 0.0 us)

commit v6 on v5

--- a/solution.py
+++ b/solution.py
@@ -87,6 +87,33 @@
         out_shape=jax.ShapeDtypeStruct((block_count, ROUNDS, 2, width, lanes), jnp.bfloat16),
     )(pairings, spectra)
 
+def regroup_kernel(x_ref, o_ref, *, group, width):
+    lane = lax.broadcasted_iota(jnp.int32, x_ref.shape[2:], 1)
+    low_lanes = lane < width
+    for g in range(group):
+        for q in range(2):
+            real_off = x_ref[g, 2 * q].astype(jnp.float32)
+            imag_off = x_ref[g, 2 * q + 1].astype(jnp.float32)
+            even = jnp.where(low_lanes, real_off, pltpu.roll(imag_off, width, 1))
+            odd = jnp.where(low_lanes, pltpu.roll(real_off, width, 1), imag_off)
+            rows = jnp.concatenate([even, odd], axis=0).astype(o_ref.dtype)
+            o_ref[g, pl.ds(q * rows.shape[0], rows.shape[0])] = rows
+
+
+def regroup_stage(pooled):
+    units, parts, chunks, lanes = pooled.shape
+    group = 8
+    kernel = functools.partial(regroup_kernel, group=group, width=lanes // 2)
+    out_rows = parts * chunks
+    return pl.pallas_call(
+        kernel,
+        grid=(units // group,),
+        in_specs=[pl.BlockSpec((group, parts, chunks, lanes), lambda i: (i, 0, 0, 0))],
+        out_specs=pl.BlockSpec((group, out_rows, lanes), lambda i: (i, 0, 0)),
+        out_shape=jax.ShapeDtypeStruct((units, out_rows, lanes), pooled.dtype),
+    )(pooled)
+
+
 def unshuffle_kernel(x_ref, o_ref, *, group, width):
     for k in range(group):
         flipped = x_ref[k].astype(jnp.float32).T
@@ -121,10 +148,9 @@
     layered = whitened.reshape(chan_count * day_count, 2 * per_piece, win_count * block_width)
     scale_value = 1.0 / math.sqrt(win_count * day_count)
     pooled = lax.all_to_all(layered, ("chan", "tm"), split_axis=0, concat_axis=0, tiled=True)
-    by_block = pooled.reshape(chan_count, day_count, 2, per_piece, win_count, block_width)
-    by_block = jnp.transpose(by_block, (0, 1, 2, 4, 3, 5)).reshape(
-        chan_count, day_count, 2 * win_count, per_piece * block_width
-    )
+    lanes = per_piece * block_width
+    split = pooled.reshape(chan_count * day_count, 2 * per_piece, win_count * block_width // lanes, lanes)
+    by_block = regroup_stage(split).reshape(chan_count, day_count, 2 * win_count, lanes)
     tiles = pair_stage(pairings, by_block, scale_value)
     rows = ROUNDS * 2 * block_width
     tiles = tiles.reshape(chan_count, rows, 1, 2 * block_width)

time: 248 us -> 246 us (level)
  local copies, waits for them, and re-layouts: 31.6 us -> 11.5 us
  Pallas kernels: 36.7 us -> 54.2 us
    pallas_call x0 -> x1, Pallas kernels: none -> 17.5 us  [regroup_stage(): pl.pallas_call(kernel, grid=(units // group,), in_specs=[pl.BlockSpec((gr...]
    transpose x1 -> x0, local copies, waits for them, and re-layouts: 11.9 us -> none  [on_device(): jnp.transpose(by_block, (0, 1, 2, 4, 3, 5))]
    reshape x2 -> x1, local copies, waits for them, and re-layouts: 11.7 us -> 4.1 us  [on_device(): pooled.reshape(chan_count * day_count, 2 * per_piece, win_count * block_w...]
where the time goes in v6:
time: 246 us; the launch traced here: 244 us
  blocking collectives  169 us (69%)
  Pallas kernels  54.2 us (22%)
  local copies, waits for them, and re-layouts  11.5 us (5%)
  matrix products  7.61 us (3%)
    all_to_all x1, blocking collectives, on_device(): lax.all_to_all(tiles, 'chan', split_axis=0, concat_axis=2, tiled=True)  102 us
    all_to_all x1, blocking collectives, on_device(): lax.all_to_all(layered, ('chan', 'tm'), split_axis=0, concat_axis=0, tile...  66.7 us
    pallas_call x1, Pallas kernels, pair_stage(): pl.pallas_call(kernel, grid_spec=pltpu.PrefetchScalarGridSpec(num_scalar_...  23.8 us
    pallas_call x1, Pallas kernels, regroup_stage(): pl.pallas_call(kernel, grid=(units // group,), in_specs=[pl.BlockSpec((gr...  17.5 us
    pallas_call x1, Pallas kernels, unshuffle_stage(): pl.pallas_call(kernel, grid=(rows // group,), in_specs=[pl.BlockSpec((gro...  13 us
    dot_general x1, matrix products, on_device(): lax.dot_general(dft_table, flat_raw, (((1,), (1,)), ((), ())), preferred_...  7.61 us

profile of v6, /device:TPU:2, one launch (start us, length us, event | category | flops | bytes accessed | tf_op | source)
XLA Modules:
  0.0 244.3 jit_solution(10344347948878575705)
XLA Ops:
  0.0 7.6 %multiply_reduce_fusion = (f32[1024]{0:T(1024)S(1)}, f32[1024,1024]{1,0:T(8,128)S(1)}) fusion(bf16[1024,2048]{1,0:T(8,128)(2,1)} %constant.9.clone, bf16[1024,2048]{1,0:T(8,128)(2,1)} %bitcast.18), kind=kOutput, calls=%fused_computation.2 | convolution fusion | flops 4297063424 | bytes 12587008 | tf_op jit(solution)/shard_map/dot_general | solution.py:143
  7.6 1.9 multiply_convert_fusion
  9.6 2.7 %reshape.28 = bf16[256,4,1024]{2,1,0:T(4,128)(2,1)S(1)} reshape(bf16[1024,1024]{1,0:T(8,128)(2,1)} %multiply_convert_fusion) | data formatting | bytes 4194304 | tf_op jit(solution)/shard_map/reshape | solution.py:148
  12.3 66.7 %all_to_all.20 = bf16[256,4,1024]{2,1,0:T(4,128)(2,1)} all-to-all(bf16[256,4,1024]{2,1,0:T(4,128)(2,1)S(1)} %reshape.28), channel_id=1, replica_groups=mesh['chan'=64,'tm'=4] {'chan','tm'}, dimensions={0} | all-to-all | bytes 4194304 | tf_op jit(solution)/shard_map/all_to_all | solution.py:150
  79.0 4.1 %reshape.29.x_ref = bf16[256,4,8,128]{3,2,1,0:T(8,128)(2,1)} reshape(bf16[256,4,1024]{2,1,0:T(4,128)(2,1)} %all_to_all.20) | data formatting | bytes 4194304 | tf_op jit(solution)/shard_map/reshape | solution.py:152
  83.1 17.5 %shard_map.37 = bf16[256,32,128]{2,1,0:T(8,128)(2,1)} custom-call(bf16[256,4,8,128]{3,2,1,0:T(8,128)(2,1)} %reshape.29.x_ref), custom_call_target="tpu_custom_call" | custom-call | tf_op jit(solution)/shard_map/pallas_call | solution.py:108
  100.5 23.8 %shard_map.38 = bf16[64,2,2,64,128]{4,3,2,1,0:T(8,128)(2,1)} custom-call(s32[2,64]{1,0:T(2,128)} %pair_ref.1, bf16[64,4,32,128]{3,2,1,0:T(8,128)(2,1)} %bitcast.17), custom_call_target="tpu_custom_call" | custom-call | tf_op jit(solution)/shard_map/pallas_call | solution.py:77
  124.3 102.4 %all_to_all.21 = bf16[64,256,1,128]{3,1,2,0:T(8,128)(2,1)S(1)} all-to-all(bf16[64,256,1,128]{3,1,2,0:T(8,128)(2,1)} %bitcast.15), channel_id=1, replica_groups=mesh['chan'=64,'tm'=4] {'chan'}, dimensions={0} | all-to-all | bytes 8388608 | tf_op jit(solution)/shard_map/all_to_all | solution.py:157
  226.7 4.6 %copy.8 = bf16[64,256,1,128]{3,0,1,2:T(8,128)(2,1)} copy(bf16[64,256,1,128]{3,1,2,0:T(8,128)(2,1)S(1)} %all_to_all.21) | data formatting | bytes 8388608 | tf_op jit(solution)/shard_map/all_to_all | solution.py:157
  231.3 13.0 %shard_map.39 = bf16[256,64,128]{2,1,0:T(8,128)(2,1)} custom-call(bf16[256,64,128]{2,1,0:T(8,128)(2,1)} %bitcast.16), custom_call_target="tpu_custom_call" | custom-call | tf_op jit(solution)/shard_map/pallas_call | solution.py:127
  (1 shorter events, 0.0 us)

commit v7 on v6

--- a/solution.py
+++ b/solution.py
@@ -90,7 +90,8 @@
 def regroup_kernel(x_ref, o_ref, *, group, width):
     lane = lax.broadcasted_iota(jnp.int32, x_ref.shape[2:], 1)
     low_lanes = lane < width
-    for g in range(group):
+
+    def body(g, carry):
         for q in range(2):
             real_off = x_ref[g, 2 * q].astype(jnp.float32)
             imag_off = x_ref[g, 2 * q + 1].astype(jnp.float32)
@@ -98,11 +99,14 @@
             odd = jnp.where(low_lanes, pltpu.roll(real_off, width, 1), imag_off)
             rows = jnp.concatenate([even, odd], axis=0).astype(o_ref.dtype)
             o_ref[g, pl.ds(q * rows.shape[0], rows.shape[0])] = rows
+        return carry
+
+    lax.fori_loop(0, group, body, 0, unroll=4)
 
 
 def regroup_stage(pooled):
     units, parts, chunks, lanes = pooled.shape
-    group = 8
+    group = 32
     kernel = functools.partial(regroup_kernel, group=group, width=lanes // 2)
     out_rows = parts * chunks
     return pl.pallas_call(
@@ -115,14 +119,17 @@
 
 
 def unshuffle_kernel(x_ref, o_ref, *, group, width):
-    for k in range(group):
+    def body(k, carry):
         flipped = x_ref[k].astype(jnp.float32).T
         o_ref[k] = jnp.concatenate([flipped[:width], flipped[width:]], axis=1).astype(o_ref.dtype)
+        return carry
+
+    lax.fori_loop(0, group, body, 0, unroll=4)
 
 
 def unshuffle_stage(received):
     rows, sources, lanes = received.shape
-    group = 16
+    group = 64
     kernel = functools.partial(unshuffle_kernel, group=group, width=lanes // 2)
     return pl.pallas_call(
         kernel,

time: 246 us -> 239 us (0.972)
  Pallas kernels: 54.2 us -> 48.4 us
    pallas_call x1, Pallas kernels: 17.5 us -> 8.09 us  [regroup_stage(): pl.pallas_call(kernel, grid=(units // group,), in_specs=[pl.BlockSpec((gr...]
    pallas_call x1, Pallas kernels: 13 us -> 16.6 us  [unshuffle_stage(): pl.pallas_call(kernel, grid=(rows // group,), in_specs=[pl.BlockSpec((gro...]
where the time goes in v7:
time: 239 us
  blocking collectives  169 us (71%)
  Pallas kernels  48.4 us (20%)
  local copies, waits for them, and re-layouts  11.5 us (5%)
  matrix products  7.61 us (3%)
    all_to_all x1, blocking collectives, on_device(): lax.all_to_all(tiles, 'chan', split_axis=0, concat_axis=2, tiled=True)  102 us
    all_to_all x1, blocking collectives, on_device(): lax.all_to_all(layered, ('chan', 'tm'), split_axis=0, concat_axis=0, tile...  66.7 us
    pallas_call x1, Pallas kernels, pair_stage(): pl.pallas_call(kernel, grid_spec=pltpu.PrefetchScalarGridSpec(num_scalar_...  23.8 us
    pallas_call x1, Pallas kernels, unshuffle_stage(): pl.pallas_call(kernel, grid=(rows // group,), in_specs=[pl.BlockSpec((gro...  16.6 us
    pallas_call x1, Pallas kernels, regroup_stage(): pl.pallas_call(kernel, grid=(units // group,), in_specs=[pl.BlockSpec((gr...  8.09 us
    dot_general x1, matrix products, on_device(): lax.dot_general(dft_table, flat_raw, (((1,), (1,)), ((), ())), preferred_...  7.61 us

profile of v7, /device:TPU:2, one launch (start us, length us, event | category | flops | bytes accessed | tf_op | source)
XLA Modules:
  0.0 238.5 jit_solution(13963544616144159247)
XLA Ops:
  0.0 7.6 %multiply_reduce_fusion = (f32[1024]{0:T(1024)S(1)}, f32[1024,1024]{1,0:T(8,128)S(1)}) fusion(bf16[1024,2048]{1,0:T(8,128)(2,1)} %constant.9.clone, bf16[1024,2048]{1,0:T(8,128)(2,1)} %bitcast.18), kind=kOutput, calls=%fused_computation.2 | convolution fusion | flops 4297063424 | bytes 12587008 | tf_op jit(solution)/shard_map/dot_general | solution.py:150
  7.6 1.9 multiply_convert_fusion
  9.6 2.7 %reshape.28 = bf16[256,4,1024]{2,1,0:T(4,128)(2,1)S(1)} reshape(bf16[1024,1024]{1,0:T(8,128)(2,1)} %multiply_convert_fusion) | data formatting | bytes 4194304 | tf_op jit(solution)/shard_map/reshape | solution.py:155
  12.3 66.7 %all_to_all.20 = bf16[256,4,1024]{2,1,0:T(4,128)(2,1)} all-to-all(bf16[256,4,1024]{2,1,0:T(4,128)(2,1)S(1)} %reshape.28), channel_id=1, replica_groups=mesh['chan'=64,'tm'=4] {'chan','tm'}, dimensions={0} | all-to-all | bytes 4194304 | tf_op jit(solution)/shard_map/all_to_all | solution.py:157
  79.0 4.1 %reshape.29.x_ref = bf16[256,4,8,128]{3,2,1,0:T(8,128)(2,1)} reshape(bf16[256,4,1024]{2,1,0:T(4,128)(2,1)} %all_to_all.20) | data formatting | bytes 4194304 | tf_op jit(solution)/shard_map/reshape | solution.py:159
  83.1 8.1 %shard_map.37 = bf16[256,32,128]{2,1,0:T(8,128)(2,1)} custom-call(bf16[256,4,8,128]{3,2,1,0:T(8,128)(2,1)} %reshape.29.x_ref), custom_call_target="tpu_custom_call" | custom-call | tf_op jit(solution)/shard_map/pallas_call | solution.py:112
  91.2 23.8 %shard_map.38 = bf16[64,2,2,64,128]{4,3,2,1,0:T(8,128)(2,1)} custom-call(s32[2,64]{1,0:T(2,128)} %pair_ref.1, bf16[64,4,32,128]{3,2,1,0:T(8,128)(2,1)} %bitcast.17), custom_call_target="tpu_custom_call" | custom-call | tf_op jit(solution)/shard_map/pallas_call | solution.py:77
  115.0 102.4 %all_to_all.21 = bf16[64,256,1,128]{3,1,2,0:T(8,128)(2,1)S(1)} all-to-all(bf16[64,256,1,128]{3,1,2,0:T(8,128)(2,1)} %bitcast.15), channel_id=1, replica_groups=mesh['chan'=64,'tm'=4] {'chan'}, dimensions={0} | all-to-all | bytes 8388608 | tf_op jit(solution)/shard_map/all_to_all | solution.py:164
  217.4 4.6 %copy.8 = bf16[64,256,1,128]{3,0,1,2:T(8,128)(2,1)} copy(bf16[64,256,1,128]{3,1,2,0:T(8,128)(2,1)S(1)} %all_to_all.21) | data formatting | bytes 8388608 | tf_op jit(solution)/shard_map/all_to_all | solution.py:164
  222.0 16.6 %shard_map.39 = bf16[256,64,128]{2,1,0:T(8,128)(2,1)} custom-call(bf16[256,64,128]{2,1,0:T(8,128)(2,1)} %bitcast.16), custom_call_target="tpu_custom_call" | custom-call | tf_op jit(solution)/shard_map/pallas_call | solution.py:134
  (1 shorter events, 0.0 us)

commit v8 on v7

--- a/solution.py
+++ b/solution.py
@@ -119,17 +119,14 @@
 
 
 def unshuffle_kernel(x_ref, o_ref, *, group, width):
-    def body(k, carry):
+    for k in range(group):
         flipped = x_ref[k].astype(jnp.float32).T
         o_ref[k] = jnp.concatenate([flipped[:width], flipped[width:]], axis=1).astype(o_ref.dtype)
-        return carry
-
-    lax.fori_loop(0, group, body, 0, unroll=4)
 
 
 def unshuffle_stage(received):
     rows, sources, lanes = received.shape
-    group = 64
+    group = 16
     kernel = functools.partial(unshuffle_kernel, group=group, width=lanes // 2)
     return pl.pallas_call(
         kernel,

time: 239 us -> 236 us (0.987)
  Pallas kernels: 48.4 us -> 44.8 us
    pallas_call x1, Pallas kernels: 16.6 us -> 13 us  [unshuffle_stage(): pl.pallas_call(kernel, grid=(rows // group,), in_specs=[pl.BlockSpec((gro...]
where the time goes in v8:
time: 236 us; the launch traced here: 235 us
  blocking collectives  169 us (72%)
  Pallas kernels  44.8 us (19%)
  local copies, waits for them, and re-layouts  11.5 us (5%)
  matrix products  7.61 us (3%)
    all_to_all x1, blocking collectives, on_device(): lax.all_to_all(tiles, 'chan', split_axis=0, concat_axis=2, tiled=True)  102 us
    all_to_all x1, blocking collectives, on_device(): lax.all_to_all(layered, ('chan', 'tm'), split_axis=0, concat_axis=0, tile...  66.7 us
    pallas_call x1, Pallas kernels, pair_stage(): pl.pallas_call(kernel, grid_spec=pltpu.PrefetchScalarGridSpec(num_scalar_...  23.8 us
    pallas_call x1, Pallas kernels, unshuffle_stage(): pl.pallas_call(kernel, grid=(rows // group,), in_specs=[pl.BlockSpec((gro...  13 us
    pallas_call x1, Pallas kernels, regroup_stage(): pl.pallas_call(kernel, grid=(units // group,), in_specs=[pl.BlockSpec((gr...  8.09 us
    dot_general x1, matrix products, on_device(): lax.dot_general(dft_table, flat_raw, (((1,), (1,)), ((), ())), preferred_...  7.61 us

profile of v8, /device:TPU:2, one launch (start us, length us, event | category | flops | bytes accessed | tf_op | source)
XLA Modules:
  0.0 234.9 jit_solution(529776063363233647)
XLA Ops:
  0.0 7.6 %multiply_reduce_fusion = (f32[1024]{0:T(1024)S(1)}, f32[1024,1024]{1,0:T(8,128)S(1)}) fusion(bf16[1024,2048]{1,0:T(8,128)(2,1)} %constant.9.clone, bf16[1024,2048]{1,0:T(8,128)(2,1)} %bitcast.18), kind=kOutput, calls=%fused_computation.2 | convolution fusion | flops 4297063424 | bytes 12587008 | tf_op jit(solution)/shard_map/dot_general | solution.py:147
  7.6 1.9 multiply_convert_fusion
  9.6 2.7 %reshape.28 = bf16[256,4,1024]{2,1,0:T(4,128)(2,1)S(1)} reshape(bf16[1024,1024]{1,0:T(8,128)(2,1)} %multiply_convert_fusion) | data formatting | bytes 4194304 | tf_op jit(solution)/shard_map/reshape | solution.py:152
  12.3 66.7 %all_to_all.20 = bf16[256,4,1024]{2,1,0:T(4,128)(2,1)} all-to-all(bf16[256,4,1024]{2,1,0:T(4,128)(2,1)S(1)} %reshape.28), channel_id=1, replica_groups=mesh['chan'=64,'tm'=4] {'chan','tm'}, dimensions={0} | all-to-all | bytes 4194304 | tf_op jit(solution)/shard_map/all_to_all | solution.py:154
  79.0 4.1 %reshape.29.x_ref = bf16[256,4,8,128]{3,2,1,0:T(8,128)(2,1)} reshape(bf16[256,4,1024]{2,1,0:T(4,128)(2,1)} %all_to_all.20) | data formatting | bytes 4194304 | tf_op jit(solution)/shard_map/reshape | solution.py:156
  83.1 8.1 %shard_map.37 = bf16[256,32,128]{2,1,0:T(8,128)(2,1)} custom-call(bf16[256,4,8,128]{3,2,1,0:T(8,128)(2,1)} %reshape.29.x_ref), custom_call_target="tpu_custom_call" | custom-call | tf_op jit(solution)/shard_map/pallas_call | solution.py:112
  91.2 23.8 %shard_map.38 = bf16[64,2,2,64,128]{4,3,2,1,0:T(8,128)(2,1)} custom-call(s32[2,64]{1,0:T(2,128)} %pair_ref.1, bf16[64,4,32,128]{3,2,1,0:T(8,128)(2,1)} %bitcast.17), custom_call_target="tpu_custom_call" | custom-call | tf_op jit(solution)/shard_map/pallas_call | solution.py:77
  115.0 102.4 %all_to_all.21 = bf16[64,256,1,128]{3,1,2,0:T(8,128)(2,1)S(1)} all-to-all(bf16[64,256,1,128]{3,1,2,0:T(8,128)(2,1)} %bitcast.15), channel_id=1, replica_groups=mesh['chan'=64,'tm'=4] {'chan'}, dimensions={0} | all-to-all | bytes 8388608 | tf_op jit(solution)/shard_map/all_to_all | solution.py:161
  217.4 4.6 %copy.8 = bf16[64,256,1,128]{3,0,1,2:T(8,128)(2,1)} copy(bf16[64,256,1,128]{3,1,2,0:T(8,128)(2,1)S(1)} %all_to_all.21) | data formatting | bytes 8388608 | tf_op jit(solution)/shard_map/all_to_all | solution.py:161
  222.0 13.0 %shard_map.39 = bf16[256,64,128]{2,1,0:T(8,128)(2,1)} custom-call(bf16[256,64,128]{2,1,0:T(8,128)(2,1)} %bitcast.16), custom_call_target="tpu_custom_call" | custom-call | tf_op jit(solution)/shard_map/pallas_call | solution.py:131
  (1 shorter events, 0.0 us)

commit v9 on v8

--- a/solution.py
+++ b/solution.py
@@ -120,7 +120,7 @@
 
 def unshuffle_kernel(x_ref, o_ref, *, group, width):
     for k in range(group):
-        flipped = x_ref[k].astype(jnp.float32).T
+        flipped = x_ref[k].T
         o_ref[k] = jnp.concatenate([flipped[:width], flipped[width:]], axis=1).astype(o_ref.dtype)
 
 

time: 236 us -> 235 us (level)
  no operation moved by 1% of the time
where the time goes in v9:
time: 235 us; the launch traced here: 234 us
  blocking collectives  169 us (72%)
  Pallas kernels  44 us (19%)
  local copies, waits for them, and re-layouts  11.5 us (5%)
  matrix products  7.61 us (3%)
    all_to_all x1, blocking collectives, on_device(): lax.all_to_all(tiles, 'chan', split_axis=0, concat_axis=2, tiled=True)  102 us
    all_to_all x1, blocking collectives, on_device(): lax.all_to_all(layered, ('chan', 'tm'), split_axis=0, concat_axis=0, tile...  66.7 us
    pallas_call x1, Pallas kernels, pair_stage(): pl.pallas_call(kernel, grid_spec=pltpu.PrefetchScalarGridSpec(num_scalar_...  23.8 us
    pallas_call x1, Pallas kernels, unshuffle_stage(): pl.pallas_call(kernel, grid=(rows // group,), in_specs=[pl.BlockSpec((gro...  12.1 us
    pallas_call x1, Pallas kernels, regroup_stage(): pl.pallas_call(kernel, grid=(units // group,), in_specs=[pl.BlockSpec((gr...  8.09 us
    dot_general x1, matrix products, on_device(): lax.dot_general(dft_table, flat_raw, (((1,), (1,)), ((), ())), preferred_...  7.61 us

profile of v9, /device:TPU:2, one launch (start us, length us, event | category | flops | bytes accessed | tf_op | source)
XLA Modules:
  0.0 234.1 jit_solution(11358495539820247761)
XLA Ops:
  0.0 7.6 %multiply_reduce_fusion = (f32[1024]{0:T(1024)S(1)}, f32[1024,1024]{1,0:T(8,128)S(1)}) fusion(bf16[1024,2048]{1,0:T(8,128)(2,1)} %constant.9.clone, bf16[1024,2048]{1,0:T(8,128)(2,1)} %bitcast.18), kind=kOutput, calls=%fused_computation.2 | convolution fusion | flops 4297063424 | bytes 12587008 | tf_op jit(solution)/shard_map/dot_general | solution.py:147
  7.6 1.9 multiply_convert_fusion
  9.6 2.7 %reshape.28 = bf16[256,4,1024]{2,1,0:T(4,128)(2,1)S(1)} reshape(bf16[1024,1024]{1,0:T(8,128)(2,1)} %multiply_convert_fusion) | data formatting | bytes 4194304 | tf_op jit(solution)/shard_map/reshape | solution.py:152
  12.3 66.7 %all_to_all.20 = bf16[256,4,1024]{2,1,0:T(4,128)(2,1)} all-to-all(bf16[256,4,1024]{2,1,0:T(4,128)(2,1)S(1)} %reshape.28), channel_id=1, replica_groups=mesh['chan'=64,'tm'=4] {'chan','tm'}, dimensions={0} | all-to-all | bytes 4194304 | tf_op jit(solution)/shard_map/all_to_all | solution.py:154
  79.0 4.1 %reshape.29.x_ref = bf16[256,4,8,128]{3,2,1,0:T(8,128)(2,1)} reshape(bf16[256,4,1024]{2,1,0:T(4,128)(2,1)} %all_to_all.20) | data formatting | bytes 4194304 | tf_op jit(solution)/shard_map/reshape | solution.py:156
  83.1 8.1 %shard_map.37 = bf16[256,32,128]{2,1,0:T(8,128)(2,1)} custom-call(bf16[256,4,8,128]{3,2,1,0:T(8,128)(2,1)} %reshape.29.x_ref), custom_call_target="tpu_custom_call" | custom-call | tf_op jit(solution)/shard_map/pallas_call | solution.py:112
  91.2 23.8 %shard_map.38 = bf16[64,2,2,64,128]{4,3,2,1,0:T(8,128)(2,1)} custom-call(s32[2,64]{1,0:T(2,128)} %pair_ref.1, bf16[64,4,32,128]{3,2,1,0:T(8,128)(2,1)} %bitcast.17), custom_call_target="tpu_custom_call" | custom-call | tf_op jit(solution)/shard_map/pallas_call | solution.py:77
  115.0 102.4 %all_to_all.21 = bf16[64,256,1,128]{3,1,2,0:T(8,128)(2,1)S(1)} all-to-all(bf16[64,256,1,128]{3,1,2,0:T(8,128)(2,1)} %bitcast.15), channel_id=1, replica_groups=mesh['chan'=64,'tm'=4] {'chan'}, dimensions={0} | all-to-all | bytes 8388608 | tf_op jit(solution)/shard_map/all_to_all | solution.py:161
  217.4 4.6 %copy.8 = bf16[64,256,1,128]{3,0,1,2:T(8,128)(2,1)} copy(bf16[64,256,1,128]{3,1,2,0:T(8,128)(2,1)S(1)} %all_to_all.21) | data formatting | bytes 8388608 | tf_op jit(solution)/shard_map/all_to_all | solution.py:161
  222.0 12.1 %shard_map.39 = bf16[256,64,128]{2,1,0:T(8,128)(2,1)} custom-call(bf16[256,64,128]{2,1,0:T(8,128)(2,1)} %bitcast.16), custom_call_target="tpu_custom_call" | custom-call | tf_op jit(solution)/shard_map/pallas_call | solution.py:131
  (1 shorter events, 0.0 us)

commit v10 on v9

--- a/solution.py
+++ b/solution.py
@@ -63,7 +63,7 @@
             o_ref[k, r, 1] = scaled[:, 2 * width:]
         return carry
 
-    lax.fori_loop(0, group, body, 0)
+    lax.fori_loop(0, group, body, 0, unroll=2)
 
 
 def pair_stage(pairings, spectra, scale_value):

time: 235 us -> 227 us (0.966)
  Pallas kernels: 44 us -> 36.1 us
    pallas_call x1, Pallas kernels: 23.8 us -> 16 us  [pair_stage(): pl.pallas_call(kernel, grid_spec=pltpu.PrefetchScalarGridSpec(num_scalar_...]
where the time goes in v10:
time: 227 us; the launch traced here: 226 us
  blocking collectives  169 us (74%)
  Pallas kernels  36.1 us (16%)
  local copies, waits for them, and re-layouts  11.5 us (5%)
  matrix products  7.61 us (3%)
    all_to_all x1, blocking collectives, on_device(): lax.all_to_all(tiles, 'chan', split_axis=0, concat_axis=2, tiled=True)  102 us
    all_to_all x1, blocking collectives, on_device(): lax.all_to_all(layered, ('chan', 'tm'), split_axis=0, concat_axis=0, tile...  66.7 us
    pallas_call x1, Pallas kernels, pair_stage(): pl.pallas_call(kernel, grid_spec=pltpu.PrefetchScalarGridSpec(num_scalar_...  16 us
    pallas_call x1, Pallas kernels, unshuffle_stage(): pl.pallas_call(kernel, grid=(rows // group,), in_specs=[pl.BlockSpec((gro...  12.1 us
    pallas_call x1, Pallas kernels, regroup_stage(): pl.pallas_call(kernel, grid=(units // group,), in_specs=[pl.BlockSpec((gr...  8.09 us
    dot_general x1, matrix products, on_device(): lax.dot_general(dft_table, flat_raw, (((1,), (1,)), ((), ())), preferred_...  7.61 us
    all_to_all x1, local copies, waits for them, and re-layouts, on_device(): lax.all_to_all(tiles, 'chan', split_axis=0, concat_axis=2, tiled=True)  4.62 us

profile of v10, /device:TPU:2, one launch (start us, length us, event | category | flops | bytes accessed | tf_op | source)
XLA Modules:
  0.0 226.3 jit_solution(13282877494216328054)
XLA Ops:
  0.0 7.6 %multiply_reduce_fusion = (f32[1024]{0:T(1024)S(1)}, f32[1024,1024]{1,0:T(8,128)S(1)}) fusion(bf16[1024,2048]{1,0:T(8,128)(2,1)} %constant.9.clone, bf16[1024,2048]{1,0:T(8,128)(2,1)} %bitcast.18), kind=kOutput, calls=%fused_computation.2 | convolution fusion | flops 4297063424 | bytes 12587008 | tf_op jit(solution)/shard_map/dot_general | solution.py:147
  7.6 1.9 multiply_convert_fusion
  9.6 2.7 %reshape.28 = bf16[256,4,1024]{2,1,0:T(4,128)(2,1)S(1)} reshape(bf16[1024,1024]{1,0:T(8,128)(2,1)} %multiply_convert_fusion) | data formatting | bytes 4194304 | tf_op jit(solution)/shard_map/reshape | solution.py:152
  12.3 66.7 %all_to_all.20 = bf16[256,4,1024]{2,1,0:T(4,128)(2,1)} all-to-all(bf16[256,4,1024]{2,1,0:T(4,128)(2,1)S(1)} %reshape.28), channel_id=1, replica_groups=mesh['chan'=64,'tm'=4] {'chan','tm'}, dimensions={0} | all-to-all | bytes 4194304 | tf_op jit(solution)/shard_map/all_to_all | solution.py:154
  79.0 4.1 %reshape.29.x_ref = bf16[256,4,8,128]{3,2,1,0:T(8,128)(2,1)} reshape(bf16[256,4,1024]{2,1,0:T(4,128)(2,1)} %all_to_all.20) | data formatting | bytes 4194304 | tf_op jit(solution)/shard_map/reshape | solution.py:156
  83.1 8.1 %shard_map.37 = bf16[256,32,128]{2,1,0:T(8,128)(2,1)} custom-call(bf16[256,4,8,128]{3,2,1,0:T(8,128)(2,1)} %reshape.29.x_ref), custom_call_target="tpu_custom_call" | custom-call | tf_op jit(solution)/shard_map/pallas_call | solution.py:112
  91.2 16.0 %shard_map.38 = bf16[64,2,2,64,128]{4,3,2,1,0:T(8,128)(2,1)} custom-call(s32[2,64]{1,0:T(2,128)} %pair_ref.1, bf16[64,4,32,128]{3,2,1,0:T(8,128)(2,1)} %bitcast.17), custom_call_target="tpu_custom_call" | custom-call | tf_op jit(solution)/shard_map/pallas_call | solution.py:77
  107.2 102.4 %all_to_all.21 = bf16[64,256,1,128]{3,1,2,0:T(8,128)(2,1)S(1)} all-to-all(bf16[64,256,1,128]{3,1,2,0:T(8,128)(2,1)} %bitcast.15), channel_id=1, replica_groups=mesh['chan'=64,'tm'=4] {'chan'}, dimensions={0} | all-to-all | bytes 8388608 | tf_op jit(solution)/shard_map/all_to_all | solution.py:161
  209.6 4.6 %copy.8 = bf16[64,256,1,128]{3,0,1,2:T(8,128)(2,1)} copy(bf16[64,256,1,128]{3,1,2,0:T(8,128)(2,1)S(1)} %all_to_all.21) | data formatting | bytes 8388608 | tf_op jit(solution)/shard_map/all_to_all | solution.py:161
  214.2 12.1 %shard_map.39 = bf16[256,64,128]{2,1,0:T(8,128)(2,1)} custom-call(bf16[256,64,128]{2,1,0:T(8,128)(2,1)} %bitcast.16), custom_call_target="tpu_custom_call" | custom-call | tf_op jit(solution)/shard_map/pallas_call | solution.py:131
  (1 shorter events, 0.0 us)

commit v11 on v10

--- a/solution.py
+++ b/solution.py
@@ -63,7 +63,7 @@
             o_ref[k, r, 1] = scaled[:, 2 * width:]
         return carry
 
-    lax.fori_loop(0, group, body, 0, unroll=2)
+    lax.fori_loop(0, group, body, 0, unroll=4)
 
 
 def pair_stage(pairings, spectra, scale_value):

time: 227 us -> 223 us (0.982)
  Pallas kernels: 36.1 us -> 32.5 us
    pallas_call x1, Pallas kernels: 16 us -> 12.3 us  [pair_stage(): pl.pallas_call(kernel, grid_spec=pltpu.PrefetchScalarGridSpec(num_scalar_...]
where the time goes in v11:
time: 223 us
  blocking collectives  169 us (76%)
  Pallas kernels  32.5 us (15%)
  local copies, waits for them, and re-layouts  11.5 us (5%)
  matrix products  7.61 us (3%)
    all_to_all x1, blocking collectives, on_device(): lax.all_to_all(tiles, 'chan', split_axis=0, concat_axis=2, tiled=True)  102 us
    all_to_all x1, blocking collectives, on_device(): lax.all_to_all(layered, ('chan', 'tm'), split_axis=0, concat_axis=0, tile...  66.7 us
    pallas_call x1, Pallas kernels, pair_stage(): pl.pallas_call(kernel, grid_spec=pltpu.PrefetchScalarGridSpec(num_scalar_...  12.3 us
    pallas_call x1, Pallas kernels, unshuffle_stage(): pl.pallas_call(kernel, grid=(rows // group,), in_specs=[pl.BlockSpec((gro...  12.1 us
    pallas_call x1, Pallas kernels, regroup_stage(): pl.pallas_call(kernel, grid=(units // group,), in_specs=[pl.BlockSpec((gr...  8.09 us
    dot_general x1, matrix products, on_device(): lax.dot_general(dft_table, flat_raw, (((1,), (1,)), ((), ())), preferred_...  7.61 us
    all_to_all x1, local copies, waits for them, and re-layouts, on_device(): lax.all_to_all(tiles, 'chan', split_axis=0, concat_axis=2, tiled=True)  4.62 us

profile of v11, /device:TPU:2, one launch (start us, length us, event | category | flops | bytes accessed | tf_op | source)
XLA Modules:
  0.0 222.7 jit_solution(4725076983539063776)
XLA Ops:
  0.0 7.6 %multiply_reduce_fusion = (f32[1024]{0:T(1024)S(1)}, f32[1024,1024]{1,0:T(8,128)S(1)}) fusion(bf16[1024,2048]{1,0:T(8,128)(2,1)} %constant.9.clone, bf16[1024,2048]{1,0:T(8,128)(2,1)} %bitcast.18), kind=kOutput, calls=%fused_computation.2 | convolution fusion | flops 4297063424 | bytes 12587008 | tf_op jit(solution)/shard_map/dot_general | solution.py:147
  7.6 1.9 multiply_convert_fusion
  9.6 2.7 %reshape.28 = bf16[256,4,1024]{2,1,0:T(4,128)(2,1)S(1)} reshape(bf16[1024,1024]{1,0:T(8,128)(2,1)} %multiply_convert_fusion) | data formatting | bytes 4194304 | tf_op jit(solution)/shard_map/reshape | solution.py:152
  12.3 66.7 %all_to_all.20 = bf16[256,4,1024]{2,1,0:T(4,128)(2,1)} all-to-all(bf16[256,4,1024]{2,1,0:T(4,128)(2,1)S(1)} %reshape.28), channel_id=1, replica_groups=mesh['chan'=64,'tm'=4] {'chan','tm'}, dimensions={0} | all-to-all | bytes 4194304 | tf_op jit(solution)/shard_map/all_to_all | solution.py:154
  79.0 4.1 %reshape.29.x_ref = bf16[256,4,8,128]{3,2,1,0:T(8,128)(2,1)} reshape(bf16[256,4,1024]{2,1,0:T(4,128)(2,1)} %all_to_all.20) | data formatting | bytes 4194304 | tf_op jit(solution)/shard_map/reshape | solution.py:156
  83.1 8.1 %shard_map.37 = bf16[256,32,128]{2,1,0:T(8,128)(2,1)} custom-call(bf16[256,4,8,128]{3,2,1,0:T(8,128)(2,1)} %reshape.29.x_ref), custom_call_target="tpu_custom_call" | custom-call | tf_op jit(solution)/shard_map/pallas_call | solution.py:112
  91.2 12.3 %shard_map.38 = bf16[64,2,2,64,128]{4,3,2,1,0:T(8,128)(2,1)} custom-call(s32[2,64]{1,0:T(2,128)} %pair_ref.1, bf16[64,4,32,128]{3,2,1,0:T(8,128)(2,1)} %bitcast.17), custom_call_target="tpu_custom_call" | custom-call | tf_op jit(solution)/shard_map/pallas_call | solution.py:77
  103.5 102.4 %all_to_all.21 = bf16[64,256,1,128]{3,1,2,0:T(8,128)(2,1)S(1)} all-to-all(bf16[64,256,1,128]{3,1,2,0:T(8,128)(2,1)} %bitcast.15), channel_id=1, replica_groups=mesh['chan'=64,'tm'=4] {'chan'}, dimensions={0} | all-to-all | bytes 8388608 | tf_op jit(solution)/shard_map/all_to_all | solution.py:161
  205.9 4.6 %copy.8 = bf16[64,256,1,128]{3,0,1,2:T(8,128)(2,1)} copy(bf16[64,256,1,128]{3,1,2,0:T(8,128)(2,1)S(1)} %all_to_all.21) | data formatting | bytes 8388608 | tf_op jit(solution)/shard_map/all_to_all | solution.py:161
  210.6 12.1 %shard_map.39 = bf16[256,64,128]{2,1,0:T(8,128)(2,1)} custom-call(bf16[256,64,128]{2,1,0:T(8,128)(2,1)} %bitcast.16), custom_call_target="tpu_custom_call" | custom-call | tf_op jit(solution)/shard_map/pallas_call | solution.py:131
  (1 shorter events, 0.0 us)

commit v12 on v11

--- a/solution.py
+++ b/solution.py
@@ -63,7 +63,7 @@
             o_ref[k, r, 1] = scaled[:, 2 * width:]
         return carry
 
-    lax.fori_loop(0, group, body, 0, unroll=4)
+    lax.fori_loop(0, group, body, 0, unroll=8)
 
 
 def pair_stage(pairings, spectra, scale_value):
@@ -101,7 +101,7 @@
             o_ref[g, pl.ds(q * rows.shape[0], rows.shape[0])] = rows
         return carry
 
-    lax.fori_loop(0, group, body, 0, unroll=4)
+    lax.fori_loop(0, group, body, 0, unroll=8)
 
 
 def regroup_stage(pooled):

time: 223 us -> 220 us (0.987)
  Pallas kernels: 32.5 us -> 29.4 us
where the time goes in v12:
time: 220 us
  blocking collectives  169 us (77%)
  Pallas kernels  29.4 us (13%)
  local copies, waits for them, and re-layouts  11.5 us (5%)
  matrix products  7.61 us (3%)
    all_to_all x1, blocking collectives, on_device(): lax.all_to_all(tiles, 'chan', split_axis=0, concat_axis=2, tiled=True)  102 us
    all_to_all x1, blocking collectives, on_device(): lax.all_to_all(layered, ('chan', 'tm'), split_axis=0, concat_axis=0, tile...  66.7 us
    pallas_call x1, Pallas kernels, unshuffle_stage(): pl.pallas_call(kernel, grid=(rows // group,), in_specs=[pl.BlockSpec((gro...  12.1 us
    pallas_call x1, Pallas kernels, pair_stage(): pl.pallas_call(kernel, grid_spec=pltpu.PrefetchScalarGridSpec(num_scalar_...  10.5 us
    dot_general x1, matrix products, on_device(): lax.dot_general(dft_table, flat_raw, (((1,), (1,)), ((), ())), preferred_...  7.61 us
    pallas_call x1, Pallas kernels, regroup_stage(): pl.pallas_call(kernel, grid=(units // group,), in_specs=[pl.BlockSpec((gr...  6.89 us
    all_to_all x1, local copies, waits for them, and re-layouts, on_device(): lax.all_to_all(tiles, 'chan', split_axis=0, concat_axis=2, tiled=True)  4.62 us

profile of v12, /device:TPU:2, one launch (start us, length us, event | category | flops | bytes accessed | tf_op | source)
XLA Modules:
  0.0 219.6 jit_solution(2210535594615133470)
XLA Ops:
  0.0 7.6 %multiply_reduce_fusion = (f32[1024]{0:T(1024)S(1)}, f32[1024,1024]{1,0:T(8,128)S(1)}) fusion(bf16[1024,2048]{1,0:T(8,128)(2,1)} %constant.9.clone, bf16[1024,2048]{1,0:T(8,128)(2,1)} %bitcast.18), kind=kOutput, calls=%fused_computation.2 | convolution fusion | flops 4297063424 | bytes 12587008 | tf_op jit(solution)/shard_map/dot_general | solution.py:147
  7.6 1.9 multiply_convert_fusion
  9.6 2.7 %reshape.28 = bf16[256,4,1024]{2,1,0:T(4,128)(2,1)S(1)} reshape(bf16[1024,1024]{1,0:T(8,128)(2,1)} %multiply_convert_fusion) | data formatting | bytes 4194304 | tf_op jit(solution)/shard_map/reshape | solution.py:152
  12.3 66.7 %all_to_all.20 = bf16[256,4,1024]{2,1,0:T(4,128)(2,1)} all-to-all(bf16[256,4,1024]{2,1,0:T(4,128)(2,1)S(1)} %reshape.28), channel_id=1, replica_groups=mesh['chan'=64,'tm'=4] {'chan','tm'}, dimensions={0} | all-to-all | bytes 4194304 | tf_op jit(solution)/shard_map/all_to_all | solution.py:154
  79.0 4.1 %reshape.29.x_ref = bf16[256,4,8,128]{3,2,1,0:T(8,128)(2,1)} reshape(bf16[256,4,1024]{2,1,0:T(4,128)(2,1)} %all_to_all.20) | data formatting | bytes 4194304 | tf_op jit(solution)/shard_map/reshape | solution.py:156
  83.1 6.9 %shard_map.37 = bf16[256,32,128]{2,1,0:T(8,128)(2,1)} custom-call(bf16[256,4,8,128]{3,2,1,0:T(8,128)(2,1)} %reshape.29.x_ref), custom_call_target="tpu_custom_call" | custom-call | tf_op jit(solution)/shard_map/pallas_call | solution.py:112
  90.0 10.5 %shard_map.38 = bf16[64,2,2,64,128]{4,3,2,1,0:T(8,128)(2,1)} custom-call(s32[2,64]{1,0:T(2,128)} %pair_ref.1, bf16[64,4,32,128]{3,2,1,0:T(8,128)(2,1)} %bitcast.17), custom_call_target="tpu_custom_call" | custom-call | tf_op jit(solution)/shard_map/pallas_call | solution.py:77
  100.4 102.4 %all_to_all.21 = bf16[64,256,1,128]{3,1,2,0:T(8,128)(2,1)S(1)} all-to-all(bf16[64,256,1,128]{3,1,2,0:T(8,128)(2,1)} %bitcast.15), channel_id=1, replica_groups=mesh['chan'=64,'tm'=4] {'chan'}, dimensions={0} | all-to-all | bytes 8388608 | tf_op jit(solution)/shard_map/all_to_all | solution.py:161
  202.8 4.6 %copy.8 = bf16[64,256,1,128]{3,0,1,2:T(8,128)(2,1)} copy(bf16[64,256,1,128]{3,1,2,0:T(8,128)(2,1)S(1)} %all_to_all.21) | data formatting | bytes 8388608 | tf_op jit(solution)/shard_map/all_to_all | solution.py:161
  207.5 12.1 %shard_map.39 = bf16[256,64,128]{2,1,0:T(8,128)(2,1)} custom-call(bf16[256,64,128]{2,1,0:T(8,128)(2,1)} %bitcast.16), custom_call_target="tpu_custom_call" | custom-call | tf_op jit(solution)/shard_map/pallas_call | solution.py:131
  (1 shorter events, 0.0 us)

commit v13 on v12

--- a/solution.py
+++ b/solution.py
@@ -126,7 +126,7 @@
 
 def unshuffle_stage(received):
     rows, sources, lanes = received.shape
-    group = 16
+    group = 32
     kernel = functools.partial(unshuffle_kernel, group=group, width=lanes // 2)
     return pl.pallas_call(
         kernel,

time: 220 us -> 216 us (0.982)
  Pallas kernels: 29.4 us -> 25.6 us
    pallas_call x1, Pallas kernels: 12.1 us -> 8.23 us  [unshuffle_stage(): pl.pallas_call(kernel, grid=(rows // group,), in_specs=[pl.BlockSpec((gro...]
where the time goes in v13:
time: 216 us
  blocking collectives  169 us (78%)
  Pallas kernels  25.6 us (12%)
  local copies, waits for them, and re-layouts  11.5 us (5%)
  matrix products  7.61 us (4%)
    all_to_all x1, blocking collectives, on_device(): lax.all_to_all(tiles, 'chan', split_axis=0, concat_axis=2, tiled=True)  102 us
    all_to_all x1, blocking collectives, on_device(): lax.all_to_all(layered, ('chan', 'tm'), split_axis=0, concat_axis=0, tile...  66.7 us
    pallas_call x1, Pallas kernels, pair_stage(): pl.pallas_call(kernel, grid_spec=pltpu.PrefetchScalarGridSpec(num_scalar_...  10.5 us
    pallas_call x1, Pallas kernels, unshuffle_stage(): pl.pallas_call(kernel, grid=(rows // group,), in_specs=[pl.BlockSpec((gro...  8.23 us
    dot_general x1, matrix products, on_device(): lax.dot_general(dft_table, flat_raw, (((1,), (1,)), ((), ())), preferred_...  7.61 us
    pallas_call x1, Pallas kernels, regroup_stage(): pl.pallas_call(kernel, grid=(units // group,), in_specs=[pl.BlockSpec((gr...  6.89 us
    all_to_all x1, local copies, waits for them, and re-layouts, on_device(): lax.all_to_all(tiles, 'chan', split_axis=0, concat_axis=2, tiled=True)  4.62 us

profile of v13, /device:TPU:2, one launch (start us, length us, event | category | flops | bytes accessed | tf_op | source)
XLA Modules:
  0.0 215.7 jit_solution(14831828184108453416)
XLA Ops:
  0.0 7.6 %multiply_reduce_fusion = (f32[1024]{0:T(1024)S(1)}, f32[1024,1024]{1,0:T(8,128)S(1)}) fusion(bf16[1024,2048]{1,0:T(8,128)(2,1)} %constant.9.clone, bf16[1024,2048]{1,0:T(8,128)(2,1)} %bitcast.18), kind=kOutput, calls=%fused_computation.2 | convolution fusion | flops 4297063424 | bytes 12587008 | tf_op jit(solution)/shard_map/dot_general | solution.py:147
  7.6 1.9 multiply_convert_fusion
  9.6 2.7 %reshape.28 = bf16[256,4,1024]{2,1,0:T(4,128)(2,1)S(1)} reshape(bf16[1024,1024]{1,0:T(8,128)(2,1)} %multiply_convert_fusion) | data formatting | bytes 4194304 | tf_op jit(solution)/shard_map/reshape | solution.py:152
  12.3 66.7 %all_to_all.20 = bf16[256,4,1024]{2,1,0:T(4,128)(2,1)} all-to-all(bf16[256,4,1024]{2,1,0:T(4,128)(2,1)S(1)} %reshape.28), channel_id=1, replica_groups=mesh['chan'=64,'tm'=4] {'chan','tm'}, dimensions={0} | all-to-all | bytes 4194304 | tf_op jit(solution)/shard_map/all_to_all | solution.py:154
  79.0 4.1 %reshape.29.x_ref = bf16[256,4,8,128]{3,2,1,0:T(8,128)(2,1)} reshape(bf16[256,4,1024]{2,1,0:T(4,128)(2,1)} %all_to_all.20) | data formatting | bytes 4194304 | tf_op jit(solution)/shard_map/reshape | solution.py:156
  83.1 6.9 %shard_map.37 = bf16[256,32,128]{2,1,0:T(8,128)(2,1)} custom-call(bf16[256,4,8,128]{3,2,1,0:T(8,128)(2,1)} %reshape.29.x_ref), custom_call_target="tpu_custom_call" | custom-call | tf_op jit(solution)/shard_map/pallas_call | solution.py:112
  90.0 10.5 %shard_map.38 = bf16[64,2,2,64,128]{4,3,2,1,0:T(8,128)(2,1)} custom-call(s32[2,64]{1,0:T(2,128)} %pair_ref.1, bf16[64,4,32,128]{3,2,1,0:T(8,128)(2,1)} %bitcast.17), custom_call_target="tpu_custom_call" | custom-call | tf_op jit(solution)/shard_map/pallas_call | solution.py:77
  100.4 102.4 %all_to_all.21 = bf16[64,256,1,128]{3,1,2,0:T(8,128)(2,1)S(1)} all-to-all(bf16[64,256,1,128]{3,1,2,0:T(8,128)(2,1)} %bitcast.15), channel_id=1, replica_groups=mesh['chan'=64,'tm'=4] {'chan'}, dimensions={0} | all-to-all | bytes 8388608 | tf_op jit(solution)/shard_map/all_to_all | solution.py:161
  202.8 4.6 %copy.8 = bf16[64,256,1,128]{3,0,1,2:T(8,128)(2,1)} copy(bf16[64,256,1,128]{3,1,2,0:T(8,128)(2,1)S(1)} %all_to_all.21) | data formatting | bytes 8388608 | tf_op jit(solution)/shard_map/all_to_all | solution.py:161
  207.5 8.2 %shard_map.39 = bf16[256,64,128]{2,1,0:T(8,128)(2,1)} custom-call(bf16[256,64,128]{2,1,0:T(8,128)(2,1)} %bitcast.16), custom_call_target="tpu_custom_call" | custom-call | tf_op jit(solution)/shard_map/pallas_call | solution.py:131
  (1 shorter events, 0.0 us)

commit v14 on v13

--- a/solution.py
+++ b/solution.py
@@ -126,7 +126,7 @@
 
 def unshuffle_stage(received):
     rows, sources, lanes = received.shape
-    group = 32
+    group = 64
     kernel = functools.partial(unshuffle_kernel, group=group, width=lanes // 2)
     return pl.pallas_call(
         kernel,

time: 216 us -> 215 us (level)
  no operation moved by 1% of the time
where the time goes in v14:
time: 215 us; the launch traced here: 214 us
  blocking collectives  169 us (79%)
  Pallas kernels  24 us (11%)
  local copies, waits for them, and re-layouts  11.5 us (5%)
  matrix products  7.61 us (4%)
    all_to_all x1, blocking collectives, on_device(): lax.all_to_all(tiles, 'chan', split_axis=0, concat_axis=2, tiled=True)  102 us
    all_to_all x1, blocking collectives, on_device(): lax.all_to_all(layered, ('chan', 'tm'), split_axis=0, concat_axis=0, tile...  66.7 us
    pallas_call x1, Pallas kernels, pair_stage(): pl.pallas_call(kernel, grid_spec=pltpu.PrefetchScalarGridSpec(num_scalar_...  10.5 us
    dot_general x1, matrix products, on_device(): lax.dot_general(dft_table, flat_raw, (((1,), (1,)), ((), ())), preferred_...  7.61 us
    pallas_call x1, Pallas kernels, regroup_stage(): pl.pallas_call(kernel, grid=(units // group,), in_specs=[pl.BlockSpec((gr...  6.89 us
    pallas_call x1, Pallas kernels, unshuffle_stage(): pl.pallas_call(kernel, grid=(rows // group,), in_specs=[pl.BlockSpec((gro...  6.63 us
    all_to_all x1, local copies, waits for them, and re-layouts, on_device(): lax.all_to_all(tiles, 'chan', split_axis=0, concat_axis=2, tiled=True)  4.62 us

profile of v14, /device:TPU:2, one launch (start us, length us, event | category | flops | bytes accessed | tf_op | source)
XLA Modules:
  0.0 214.1 jit_solution(5915668457798276784)
XLA Ops:
  0.0 7.6 %multiply_reduce_fusion = (f32[1024]{0:T(1024)S(1)}, f32[1024,1024]{1,0:T(8,128)S(1)}) fusion(bf16[1024,2048]{1,0:T(8,128)(2,1)} %constant.9.clone, bf16[1024,2048]{1,0:T(8,128)(2,1)} %bitcast.18), kind=kOutput, calls=%fused_computation.2 | convolution fusion | flops 4297063424 | bytes 12587008 | tf_op jit(solution)/shard_map/dot_general | solution.py:147
  7.6 1.9 multiply_convert_fusion
  9.6 2.7 %reshape.28 = bf16[256,4,1024]{2,1,0:T(4,128)(2,1)S(1)} reshape(bf16[1024,1024]{1,0:T(8,128)(2,1)} %multiply_convert_fusion) | data formatting | bytes 4194304 | tf_op jit(solution)/shard_map/reshape | solution.py:152
  12.3 66.7 %all_to_all.20 = bf16[256,4,1024]{2,1,0:T(4,128)(2,1)} all-to-all(bf16[256,4,1024]{2,1,0:T(4,128)(2,1)S(1)} %reshape.28), channel_id=1, replica_groups=mesh['chan'=64,'tm'=4] {'chan','tm'}, dimensions={0} | all-to-all | bytes 4194304 | tf_op jit(solution)/shard_map/all_to_all | solution.py:154
  79.0 4.1 %reshape.29.x_ref = bf16[256,4,8,128]{3,2,1,0:T(8,128)(2,1)} reshape(bf16[256,4,1024]{2,1,0:T(4,128)(2,1)} %all_to_all.20) | data formatting | bytes 4194304 | tf_op jit(solution)/shard_map/reshape | solution.py:156
  83.1 6.9 %shard_map.37 = bf16[256,32,128]{2,1,0:T(8,128)(2,1)} custom-call(bf16[256,4,8,128]{3,2,1,0:T(8,128)(2,1)} %reshape.29.x_ref), custom_call_target="tpu_custom_call" | custom-call | tf_op jit(solution)/shard_map/pallas_call | solution.py:112
  90.0 10.5 %shard_map.38 = bf16[64,2,2,64,128]{4,3,2,1,0:T(8,128)(2,1)} custom-call(s32[2,64]{1,0:T(2,128)} %pair_ref.1, bf16[64,4,32,128]{3,2,1,0:T(8,128)(2,1)} %bitcast.17), custom_call_target="tpu_custom_call" | custom-call | tf_op jit(solution)/shard_map/pallas_call | solution.py:77
  100.4 102.4 %all_to_all.21 = bf16[64,256,1,128]{3,1,2,0:T(8,128)(2,1)S(1)} all-to-all(bf16[64,256,1,128]{3,1,2,0:T(8,128)(2,1)} %bitcast.15), channel_id=1, replica_groups=mesh['chan'=64,'tm'=4] {'chan'}, dimensions={0} | all-to-all | bytes 8388608 | tf_op jit(solution)/shard_map/all_to_all | solution.py:161
  202.8 4.6 %copy.8 = bf16[64,256,1,128]{3,0,1,2:T(8,128)(2,1)} copy(bf16[64,256,1,128]{3,1,2,0:T(8,128)(2,1)S(1)} %all_to_all.21) | data formatting | bytes 8388608 | tf_op jit(solution)/shard_map/all_to_all | solution.py:161
  207.5 6.6 %shard_map.39 = bf16[256,64,128]{2,1,0:T(8,128)(2,1)} custom-call(bf16[256,64,128]{2,1,0:T(8,128)(2,1)} %bitcast.16), custom_call_target="tpu_custom_call" | custom-call | tf_op jit(solution)/shard_map/pallas_call | solution.py:131
  (1 shorter events, 0.0 us)

commit v15 on v14

--- a/solution.py
+++ b/solution.py
@@ -106,7 +106,7 @@
 
 def regroup_stage(pooled):
     units, parts, chunks, lanes = pooled.shape
-    group = 32
+    group = 64
     kernel = functools.partial(regroup_kernel, group=group, width=lanes // 2)
     out_rows = parts * chunks
     return pl.pallas_call(

time: 215 us -> 213 us (level)
  no operation moved by 1% of the time
where the time goes in v15:
time: 213 us; the launch traced here: 212 us
  blocking collectives  169 us (79%)
  Pallas kernels  22.4 us (11%)
  local copies, waits for them, and re-layouts  11.5 us (5%)
  matrix products  7.61 us (4%)
    all_to_all x1, blocking collectives, on_device(): lax.all_to_all(tiles, 'chan', split_axis=0, concat_axis=2, tiled=True)  102 us
    all_to_all x1, blocking collectives, on_device(): lax.all_to_all(layered, ('chan', 'tm'), split_axis=0, concat_axis=0, tile...  66.7 us
    pallas_call x1, Pallas kernels, pair_stage(): pl.pallas_call(kernel, grid_spec=pltpu.PrefetchScalarGridSpec(num_scalar_...  10.5 us
    dot_general x1, matrix products, on_device(): lax.dot_general(dft_table, flat_raw, (((1,), (1,)), ((), ())), preferred_...  7.61 us
    pallas_call x1, Pallas kernels, unshuffle_stage(): pl.pallas_call(kernel, grid=(rows // group,), in_specs=[pl.BlockSpec((gro...  6.63 us
    pallas_call x1, Pallas kernels, regroup_stage(): pl.pallas_call(kernel, grid=(units // group,), in_specs=[pl.BlockSpec((gr...  5.27 us
    all_to_all x1, local copies, waits for them, and re-layouts, on_device(): lax.all_to_all(tiles, 'chan', split_axis=0, concat_axis=2, tiled=True)  4.62 us

profile of v15, /device:TPU:2, one launch (start us, length us, event | category | flops | bytes accessed | tf_op | source)
XLA Modules:
  0.0 212.5 jit_solution(18282700580339861346)
XLA Ops:
  0.0 7.6 %multiply_reduce_fusion = (f32[1024]{0:T(1024)S(1)}, f32[1024,1024]{1,0:T(8,128)S(1)}) fusion(bf16[1024,2048]{1,0:T(8,128)(2,1)} %constant.9.clone, bf16[1024,2048]{1,0:T(8,128)(2,1)} %bitcast.18), kind=kOutput, calls=%fused_computation.2 | convolution fusion | flops 4297063424 | bytes 12587008 | tf_op jit(solution)/shard_map/dot_general | solution.py:147
  7.6 1.9 multiply_convert_fusion
  9.6 2.7 %reshape.28 = bf16[256,4,1024]{2,1,0:T(4,128)(2,1)S(1)} reshape(bf16[1024,1024]{1,0:T(8,128)(2,1)} %multiply_convert_fusion) | data formatting | bytes 4194304 | tf_op jit(solution)/shard_map/reshape | solution.py:152
  12.3 66.7 %all_to_all.20 = bf16[256,4,1024]{2,1,0:T(4,128)(2,1)} all-to-all(bf16[256,4,1024]{2,1,0:T(4,128)(2,1)S(1)} %reshape.28), channel_id=1, replica_groups=mesh['chan'=64,'tm'=4] {'chan','tm'}, dimensions={0} | all-to-all | bytes 4194304 | tf_op jit(solution)/shard_map/all_to_all | solution.py:154
  79.0 4.1 %reshape.29.x_ref = bf16[256,4,8,128]{3,2,1,0:T(8,128)(2,1)} reshape(bf16[256,4,1024]{2,1,0:T(4,128)(2,1)} %all_to_all.20) | data formatting | bytes 4194304 | tf_op jit(solution)/shard_map/reshape | solution.py:156
  83.1 5.3 %shard_map.37 = bf16[256,32,128]{2,1,0:T(8,128)(2,1)} custom-call(bf16[256,4,8,128]{3,2,1,0:T(8,128)(2,1)} %reshape.29.x_ref), custom_call_target="tpu_custom_call" | custom-call | tf_op jit(solution)/shard_map/pallas_call | solution.py:112
  88.4 10.5 %shard_map.38 = bf16[64,2,2,64,128]{4,3,2,1,0:T(8,128)(2,1)} custom-call(s32[2,64]{1,0:T(2,128)} %pair_ref.1, bf16[64,4,32,128]{3,2,1,0:T(8,128)(2,1)} %bitcast.17), custom_call_target="tpu_custom_call" | custom-call | tf_op jit(solution)/shard_map/pallas_call | solution.py:77
  98.8 102.4 %all_to_all.21 = bf16[64,256,1,128]{3,1,2,0:T(8,128)(2,1)S(1)} all-to-all(bf16[64,256,1,128]{3,1,2,0:T(8,128)(2,1)} %bitcast.15), channel_id=1, replica_groups=mesh['chan'=64,'tm'=4] {'chan'}, dimensions={0} | all-to-all | bytes 8388608 | tf_op jit(solution)/shard_map/all_to_all | solution.py:161
  201.2 4.6 %copy.8 = bf16[64,256,1,128]{3,0,1,2:T(8,128)(2,1)} copy(bf16[64,256,1,128]{3,1,2,0:T(8,128)(2,1)S(1)} %all_to_all.21) | data formatting | bytes 8388608 | tf_op jit(solution)/shard_map/all_to_all | solution.py:161
  205.9 6.6 %shard_map.39 = bf16[256,64,128]{2,1,0:T(8,128)(2,1)} custom-call(bf16[256,64,128]{2,1,0:T(8,128)(2,1)} %bitcast.16), custom_call_target="tpu_custom_call" | custom-call | tf_op jit(solution)/shard_map/pallas_call | solution.py:131
  (1 shorter events, 0.0 us)

commit v16 on v15

--- a/solution.py
+++ b/solution.py
@@ -69,7 +69,7 @@
 def pair_stage(pairings, spectra, scale_value):
     block_count, day_count, rows, lanes = spectra.shape
     width = lanes // 2
-    group = 8
+    group = 16
     kernel = functools.partial(
         pair_kernel, group=group, day_count=day_count, half=rows // 2, width=width,
         scale_value=scale_value,

time: 213 us -> 213 us (level)
  no operation moved by 1% of the time
where the time goes in v16:
time: 213 us; the launch traced here: 212 us
  blocking collectives  169 us (79%)
  Pallas kernels  22.4 us (11%)
  local copies, waits for them, and re-layouts  11.5 us (5%)
  matrix products  7.61 us (4%)
    all_to_all x1, blocking collectives, on_device(): lax.all_to_all(tiles, 'chan', split_axis=0, concat_axis=2, tiled=True)  102 us
    all_to_all x1, blocking collectives, on_device(): lax.all_to_all(layered, ('chan', 'tm'), split_axis=0, concat_axis=0, tile...  66.7 us
    pallas_call x1, Pallas kernels, pair_stage(): pl.pallas_call(kernel, grid_spec=pltpu.PrefetchScalarGridSpec(num_scalar_...  10.5 us
    dot_general x1, matrix products, on_device(): lax.dot_general(dft_table, flat_raw, (((1,), (1,)), ((), ())), preferred_...  7.61 us
    pallas_call x1, Pallas kernels, unshuffle_stage(): pl.pallas_call(kernel, grid=(rows // group,), in_specs=[pl.BlockSpec((gro...  6.63 us
    pallas_call x1, Pallas kernels, regroup_stage(): pl.pallas_call(kernel, grid=(units // group,), in_specs=[pl.BlockSpec((gr...  5.27 us
    all_to_all x1, local copies, waits for them, and re-layouts, on_device(): lax.all_to_all(tiles, 'chan', split_axis=0, concat_axis=2, tiled=True)  4.62 us

profile of v16, /device:TPU:2, one launch (start us, length us, event | category | flops | bytes accessed | tf_op | source)
XLA Modules:
  0.0 212.5 jit_solution(12018360297492270477)
XLA Ops:
  0.0 7.6 %multiply_reduce_fusion = (f32[1024]{0:T(1024)S(1)}, f32[1024,1024]{1,0:T(8,128)S(1)}) fusion(bf16[1024,2048]{1,0:T(8,128)(2,1)} %constant.9.clone, bf16[1024,2048]{1,0:T(8,128)(2,1)} %bitcast.18), kind=kOutput, calls=%fused_computation.2 | convolution fusion | flops 4297063424 | bytes 12587008 | tf_op jit(solution)/shard_map/dot_general | solution.py:147
  7.6 1.9 multiply_convert_fusion
  9.6 2.7 %reshape.28 = bf16[256,4,1024]{2,1,0:T(4,128)(2,1)S(1)} reshape(bf16[1024,1024]{1,0:T(8,128)(2,1)} %multiply_convert_fusion) | data formatting | bytes 4194304 | tf_op jit(solution)/shard_map/reshape | solution.py:152
  12.3 66.7 %all_to_all.20 = bf16[256,4,1024]{2,1,0:T(4,128)(2,1)} all-to-all(bf16[256,4,1024]{2,1,0:T(4,128)(2,1)S(1)} %reshape.28), channel_id=1, replica_groups=mesh['chan'=64,'tm'=4] {'chan','tm'}, dimensions={0} | all-to-all | bytes 4194304 | tf_op jit(solution)/shard_map/all_to_all | solution.py:154
  79.0 4.1 %reshape.29.x_ref = bf16[256,4,8,128]{3,2,1,0:T(8,128)(2,1)} reshape(bf16[256,4,1024]{2,1,0:T(4,128)(2,1)} %all_to_all.20) | data formatting | bytes 4194304 | tf_op jit(solution)/shard_map/reshape | solution.py:156
  83.1 5.3 %shard_map.37 = bf16[256,32,128]{2,1,0:T(8,128)(2,1)} custom-call(bf16[256,4,8,128]{3,2,1,0:T(8,128)(2,1)} %reshape.29.x_ref), custom_call_target="tpu_custom_call" | custom-call | tf_op jit(solution)/shard_map/pallas_call | solution.py:112
  88.4 10.5 %shard_map.38 = bf16[64,2,2,64,128]{4,3,2,1,0:T(8,128)(2,1)} custom-call(s32[2,64]{1,0:T(2,128)} %pair_ref.1, bf16[64,4,32,128]{3,2,1,0:T(8,128)(2,1)} %bitcast.17), custom_call_target="tpu_custom_call" | custom-call | tf_op jit(solution)/shard_map/pallas_call | solution.py:77
  98.8 102.4 %all_to_all.21 = bf16[64,256,1,128]{3,1,2,0:T(8,128)(2,1)S(1)} all-to-all(bf16[64,256,1,128]{3,1,2,0:T(8,128)(2,1)} %bitcast.15), channel_id=1, replica_groups=mesh['chan'=64,'tm'=4] {'chan'}, dimensions={0} | all-to-all | bytes 8388608 | tf_op jit(solution)/shard_map/all_to_all | solution.py:161
  201.2 4.6 %copy.8 = bf16[64,256,1,128]{3,0,1,2:T(8,128)(2,1)} copy(bf16[64,256,1,128]{3,1,2,0:T(8,128)(2,1)S(1)} %all_to_all.21) | data formatting | bytes 8388608 | tf_op jit(solution)/shard_map/all_to_all | solution.py:161
  205.9 6.6 %shard_map.39 = bf16[256,64,128]{2,1,0:T(8,128)(2,1)} custom-call(bf16[256,64,128]{2,1,0:T(8,128)(2,1)} %bitcast.16), custom_call_target="tpu_custom_call" | custom-call | tf_op jit(solution)/shard_map/pallas_call | solution.py:131
  (1 shorter events, 0.0 us)

commit v17 on v15

--- a/solution.py
+++ b/solution.py
@@ -101,7 +101,7 @@
             o_ref[g, pl.ds(q * rows.shape[0], rows.shape[0])] = rows
         return carry
 
-    lax.fori_loop(0, group, body, 0, unroll=8)
+    lax.fori_loop(0, group, body, 0, unroll=16)
 
 
 def regroup_stage(pooled):

time: 213 us -> 212 us (level)
  no operation moved by 1% of the time
where the time goes in v17:
time: 212 us
  blocking collectives  169 us (80%)
  Pallas kernels  21.6 us (10%)
  local copies, waits for them, and re-layouts  11.5 us (5%)
  matrix products  7.61 us (4%)
    all_to_all x1, blocking collectives, on_device(): lax.all_to_all(tiles, 'chan', split_axis=0, concat_axis=2, tiled=True)  102 us
    all_to_all x1, blocking collectives, on_device(): lax.all_to_all(layered, ('chan', 'tm'), split_axis=0, concat_axis=0, tile...  66.7 us
    pallas_call x1, Pallas kernels, pair_stage(): pl.pallas_call(kernel, grid_spec=pltpu.PrefetchScalarGridSpec(num_scalar_...  10.5 us
    dot_general x1, matrix products, on_device(): lax.dot_general(dft_table, flat_raw, (((1,), (1,)), ((), ())), preferred_...  7.61 us
    pallas_call x1, Pallas kernels, unshuffle_stage(): pl.pallas_call(kernel, grid=(rows // group,), in_specs=[pl.BlockSpec((gro...  6.63 us
    all_to_all x1, local copies, waits for them, and re-layouts, on_device(): lax.all_to_all(tiles, 'chan', split_axis=0, concat_axis=2, tiled=True)  4.62 us
    pallas_call x1, Pallas kernels, regroup_stage(): pl.pallas_call(kernel, grid=(units // group,), in_specs=[pl.BlockSpec((gr...  4.56 us

profile of v17, /device:TPU:2, one launch (start us, length us, event | category | flops | bytes accessed | tf_op | source)
XLA Modules:
  0.0 211.8 jit_solution(16612209456487680231)
XLA Ops:
  0.0 7.6 %multiply_reduce_fusion = (f32[1024]{0:T(1024)S(1)}, f32[1024,1024]{1,0:T(8,128)S(1)}) fusion(bf16[1024,2048]{1,0:T(8,128)(2,1)} %constant.9.clone, bf16[1024,2048]{1,0:T(8,128)(2,1)} %bitcast.18), kind=kOutput, calls=%fused_computation.2 | convolution fusion | flops 4297063424 | bytes 12587008 | tf_op jit(solution)/shard_map/dot_general | solution.py:147
  7.6 1.9 multiply_convert_fusion
  9.6 2.7 %reshape.28 = bf16[256,4,1024]{2,1,0:T(4,128)(2,1)S(1)} reshape(bf16[1024,1024]{1,0:T(8,128)(2,1)} %multiply_convert_fusion) | data formatting | bytes 4194304 | tf_op jit(solution)/shard_map/reshape | solution.py:152
  12.3 66.7 %all_to_all.20 = bf16[256,4,1024]{2,1,0:T(4,128)(2,1)} all-to-all(bf16[256,4,1024]{2,1,0:T(4,128)(2,1)S(1)} %reshape.28), channel_id=1, replica_groups=mesh['chan'=64,'tm'=4] {'chan','tm'}, dimensions={0} | all-to-all | bytes 4194304 | tf_op jit(solution)/shard_map/all_to_all | solution.py:154
  79.0 4.1 %reshape.29.x_ref = bf16[256,4,8,128]{3,2,1,0:T(8,128)(2,1)} reshape(bf16[256,4,1024]{2,1,0:T(4,128)(2,1)} %all_to_all.20) | data formatting | bytes 4194304 | tf_op jit(solution)/shard_map/reshape | solution.py:156
  83.1 4.6 %shard_map.37 = bf16[256,32,128]{2,1,0:T(8,128)(2,1)} custom-call(bf16[256,4,8,128]{3,2,1,0:T(8,128)(2,1)} %reshape.29.x_ref), custom_call_target="tpu_custom_call" | custom-call | tf_op jit(solution)/shard_map/pallas_call | solution.py:112
  87.7 10.5 %shard_map.38 = bf16[64,2,2,64,128]{4,3,2,1,0:T(8,128)(2,1)} custom-call(s32[2,64]{1,0:T(2,128)} %pair_ref.1, bf16[64,4,32,128]{3,2,1,0:T(8,128)(2,1)} %bitcast.17), custom_call_target="tpu_custom_call" | custom-call | tf_op jit(solution)/shard_map/pallas_call | solution.py:77
  98.1 102.4 %all_to_all.21 = bf16[64,256,1,128]{3,1,2,0:T(8,128)(2,1)S(1)} all-to-all(bf16[64,256,1,128]{3,1,2,0:T(8,128)(2,1)} %bitcast.15), channel_id=1, replica_groups=mesh['chan'=64,'tm'=4] {'chan'}, dimensions={0} | all-to-all | bytes 8388608 | tf_op jit(solution)/shard_map/all_to_all | solution.py:161
  200.5 4.6 %copy.8 = bf16[64,256,1,128]{3,0,1,2:T(8,128)(2,1)} copy(bf16[64,256,1,128]{3,1,2,0:T(8,128)(2,1)S(1)} %all_to_all.21) | data formatting | bytes 8388608 | tf_op jit(solution)/shard_map/all_to_all | solution.py:161
  205.1 6.6 %shard_map.39 = bf16[256,64,128]{2,1,0:T(8,128)(2,1)} custom-call(bf16[256,64,128]{2,1,0:T(8,128)(2,1)} %bitcast.16), custom_call_target="tpu_custom_call" | custom-call | tf_op jit(solution)/shard_map/pallas_call | solution.py:131
  (1 shorter events, 0.0 us)
